TPU v7x, 32 devices: a whole 2x2x4 slice. The times are simulated.
32 devices in a mesh: tok: 4 (over y, x), voc: 8 (over z, core).
Axes of the slice: x: 2, y: 2, z: 4, core: 2. Of those that a mesh axis runs over, the one named last changes fastest.
Arguments:
- hidden: bfloat16 [8192, 2048], P(('tok', 'voc')), as said below
- gain: bfloat16 [2048], replicated, may hold values from 0.5 to 1.5
- head: bfloat16 [2048, 50304], P(None, 'voc')
- targets: int32 [8192], replicated, may hold values from 0 to 50303
- lengths: int32 [8], replicated, may hold values from 1 to 1024, 5120 in all
- perm: int32 [8], replicated, may hold values from 0 to 7, each once
Outputs:
- logprob: float32 [5120], P(('tok', 'voc'))
- entropy: float32 [5120], P(('tok', 'voc'))
Inputs may be any that keep to these rules, and one draw needn't show every extreme that they name: Each request has at least one token and the longest has exactly 1024; the lengths sum to 5120. `perm`: each request is held by exactly one slot. `hidden`: rows past a request's length in its slot are not read by any output.
All inputs are finite; a program needn't handle non-finite values.
Results may differ from a plain program's by a relative error of at most 0.0024.
Values may be sent and summed in bfloat16 or wider, within the bound.
No kernel may reach another device: no remote copies, remote signals or barrier semaphores. Data moves between devices by JAX's collectives and lax.ppermute only.
A program may use at most 256 MiB of HBM per device.

v0:
```python
import jax
import jax.numpy as jnp
from jax import lax
from jax.sharding import PartitionSpec as P

MAXLEN = 1024


def slot_rows(positions, lengths, perm):
    count = lengths.shape[0]
    ident = jnp.arange(count, dtype=jnp.int32)
    starts = jnp.cumsum(lengths) - lengths
    request = jnp.sum((positions[:, None] >= starts[None, :]).astype(jnp.int32), axis=1) - 1
    start_of = jnp.sum(jnp.where(ident[None, :] == request[:, None], starts[None, :], 0), axis=1)
    slot_of = jnp.sum(jnp.where(perm[None, :] == request[:, None], ident[None, :], 0), axis=1)
    return slot_of * MAXLEN + positions - start_of


def row_stats(piece, weights, wanted):
    logits = jnp.dot(piece, weights, preferred_element_type=jnp.float32)
    top = jnp.max(logits, axis=1)
    expo = jnp.exp(logits - top[:, None])
    total = jnp.sum(expo, axis=1)
    moment = jnp.sum(expo * logits, axis=1)
    columns = jnp.arange(logits.shape[1], dtype=jnp.int32)
    picked = jnp.sum(jnp.where(columns[None, :] == wanted[:, None], logits, 0.0), axis=1)
    return jnp.stack([top, total, moment, picked], axis=0)


def make_stats(weights, col_base, row_base, targets, slot_len):
    count = slot_len.shape[0]
    ident = jnp.arange(count, dtype=jnp.int32)

    def compute(piece, start):
        size = piece.shape[0]
        rows = row_base + jnp.arange(size, dtype=jnp.int32)
        slot = rows // MAXLEN
        row_len = jnp.sum(jnp.where(slot[:, None] == ident[None, :], slot_len[None, :], 0), axis=1)
        live = rows % MAXLEN < row_len
        wanted = lax.dynamic_slice_in_dim(targets, row_base, size, 0) - col_base

        def busy(operand):
            return row_stats(piece, weights, wanted)

        def quiet(operand):
            zeros = jnp.zeros((size,), jnp.float32)
            return jnp.stack([zeros, zeros + 1.0, zeros, zeros], axis=0)

        return lax.cond(jnp.any(live), busy, quiet, 0)

    return compute


def finish(top, total, moment, picked):
    lse = top + jnp.log(total)
    return (picked - lse, lse - moment / total)


def on_device(hidden, gain, head, targets, lengths, perm):
    values = hidden.astype(jnp.float32)
    scale = lax.rsqrt(jnp.mean(values * values, axis=1, keepdims=True) + 1e-06)
    normed = (values * scale * gain.astype(jnp.float32)[None, :]).astype(jnp.bfloat16)
    count = lengths.shape[0]
    ident = jnp.arange(count, dtype=jnp.int32)
    slot_len = jnp.sum(jnp.where(perm[:, None] == ident[None, :], lengths[None, :], 0), axis=1)
    n_tok = lax.axis_size("tok")
    n_voc = lax.axis_size("voc")
    shard_cols = head.shape[1]
    voc_index = lax.axis_index("voc")
    tok_index = lax.axis_index("tok")
    out_rows = count * MAXLEN * 5 // 8 // (n_tok * n_voc)
    device = lax.axis_index(("tok", "voc"))
    group_rows = normed.shape[0] * n_voc
    compute = make_stats(head, voc_index * shard_cols, tok_index * group_rows, targets, slot_len)
    stats = compute(lax.all_gather(normed, "voc", axis=0, tiled=True), jnp.int32(0))
    top = lax.pmax(stats[0], "voc")
    factor = jnp.exp(stats[0] - top)
    total, moment, picked = lax.psum((stats[1] * factor, stats[2] * factor, stats[3]), "voc")
    own_lp, own_ent = finish(top, total, moment, picked)
    row_logprob, row_entropy = (
        lax.all_gather(own_lp, "tok", axis=0, tiled=True),
        lax.all_gather(own_ent, "tok", axis=0, tiled=True),
    )
    positions = device * out_rows + jnp.arange(out_rows, dtype=jnp.int32)
    rows = slot_rows(positions, lengths, perm)
    return (row_logprob[rows], row_entropy[rows])


def solution(mesh):
    in_specs = (P(("tok", "voc"), None), P(), P(None, "voc"), P(), P(), P())
    out_specs = (P(("tok", "voc")), P(("tok", "voc")))
    return jax.shard_map(
        on_device, mesh=mesh, in_specs=in_specs, out_specs=out_specs, check_vma=False
    )
```

profile of v0, /device:TPU:0, one launch (start us, length us, event | category | flops | bytes accessed | tf_op | source)
XLA Modules:
  0.0 252.4 jit_solution(14086592134587553559)
XLA Ops:
  7.2 0.0 all-gather.2.cloned.1.call-start
  7.2 0.7 convert_element_type.17
  7.9 1.5 fusion.1
  9.4 2.5 %fusion.3 = bf16[256,2048]{1,0:T(8,128)(2,1)} fusion(bf16[256,2048]{1,0:T(8,128)(2,1)} %param.8, f32[2048]{0:T(1024)S(1)} %convert_element_type.17, f32[256]{0:T(256)S(1)} %add_rsqrt_fusion), kind=kLoop, calls=%fused_computation.13 | loop fusion | flops 2097152 | bytes 2106368 | tf_op jit(solution)/shard_map/convert_element_type | solution.py:62
  11.9 0.0 all-gather.2.cloned.1.call-update
  12.0 0.9 select_reduce_fusion.4
  12.9 0.1 select_reduce_fusion.1
  12.9 0.6 fusion.10
  14.2 0.8 reduce-window.9
  15.1 0.7 bitcast_subtract_fusion
  15.7 0.1 convert_reduce_fusion
  15.8 0.7 select_reduce_fusion.3
  16.6 80.3 %all-gather.2.cloned.1.call-done = bf16[2048,2048]{1,0:T(8,128)(2,1)} async-done(((bf16[256,2048]{1,0:T(8,128)(2,1)}), bf16[2048,2048]{1,0:T(8,128)(2,1)}) %all-gather.2.cloned.1.call-update) | async-done | bytes 8388624 | tf_op jit(solution)/shard_map/all_gather | solution.py:75
  96.9 87.8 %conditional.1 = (f32[4,2048]{1,0:T(4,128)S(1)}) conditional(s32[]{:T(128)} %convert_element_type.15, () %tuple.17, (bf16[2048,2048]{1,0:T(8,128)(2,1)}, bf16[2048,6288]{0,1:T(8,128)(2,1)}, s32[]{:T(128)}, s32[8192]{0:T(1024)}, s32[]{:T(128)}) %tuple.18), branch_computations={%region_4.5_spmd, %region_5.10_spmd} | conditional | flops 52850606080 | bytes 137297984 | solution.py:49
  96.9 0.8 dynamic-slice_subtract_fusion
  97.7 63.0 %fusion.14 = (f32[2048]{0:T(1024)S(1)}, f32[2048,6288]{0,1:T(8,128)}) fusion(bf16[2048,2048]{1,0:T(8,128)(2,1)} %get-tuple-element.43, bf16[2048,6288]{0,1:T(8,128)(2,1)} %get-tuple-element.70), kind=kOutput, calls=%fused_computation.49 | convolution fusion | flops 52760444928 | bytes 85663744 | tf_op jit(solution)/shard_map/cond/branch_1_fun/dot_general | solution.py:20
  160.7 23.9 %fusion = (f32[2048]{0:T(1024)S(1)}, f32[2048]{0:T(1024)S(1)}, f32[2048]{0:T(1024)S(1)}) fusion(f32[2048,6288]{0,1:T(8,128)} %get-tuple-element.83, f32[2048]{0:T(1024)S(1)} %get-tuple-element.82, s32[2048]{0:T(1024)S(1)} %dynamic-slice_subtract_fusion), kind=kLoop, calls=%fused_computation.6 | loop fusion | flops 90138624 | bytes 51552256 | tf_op jit(solution)/shard_map/cond/branch_1_fun/reduce_sum | solution.py:23
  184.7 14.3 %pmax.7 = f32[2048]{0:T(1024)S(1)} all-reduce(f32[2048]{0:T(1024)S(1)} %bitcast.16), channel_id=1, replica_groups=mesh['tok'=4,'voc'=8] {'voc'}, use_global_device_ids=true, to_apply=%region_11.12 | all-reduce | flops 2048 | bytes 16384 | tf_op jit(solution)/shard_map/pmax | solution.py:76
  199.0 26.0 %all-reduce = (f32[2048]{0:T(1024)S(1)}, f32[2048]{0:T(1024)S(1)}, f32[2048]{0:T(1024)S(1)}) all-reduce(f32[2048]{0:T(1024)S(1)} %bitcast.22, f32[2048]{0:T(1024)S(1)} %get-tuple-element.91, f32[2048]{0:T(1024)S(1)} %get-tuple-element.90), channel_id=1, replica_groups=mesh['tok'=4,'voc'=8] {'voc'}, use_global_device_ids=true, to_apply=%region_10.11 | all-reduce | flops 6144 | bytes 49152 | tf_op jit(solution)/shard_map/psum | solution.py:78
  225.0 8.3 %all_gather.11 = f32[8192]{0:T(1024)S(1)} all-gather(f32[2048]{0:T(1024)S(1)} %get-tuple-element.88), channel_id=1, replica_groups=mesh['tok'=4,'voc'=8] {'tok'}, dimensions={0}, use_global_device_ids=true | all-gather | bytes 40960 | tf_op jit(solution)/shard_map/all_gather | solution.py:82
  233.3 8.1 %all_gather.10 = f32[8192]{0:T(1024)S(1)} all-gather(f32[2048]{0:T(1024)S(1)} %get-tuple-element.89), channel_id=1, replica_groups=mesh['tok'=4,'voc'=8] {'tok'}, dimensions={0}, use_global_device_ids=true | all-gather | bytes 40960 | tf_op jit(solution)/shard_map/all_gather | solution.py:81
  241.5 2.0 gather_fusion.1
  243.5 2.0 gather_fusion
  (11 shorter events, 0.1 us)
Async XLA Ops:
  7.2 89.7 %all-gather.2.cloned.1.call-start = ((), (), s32[]{:S(2)}) async-start(), calls=%async_computation | async-start | bytes 9437184 | tf_op jit(solution)/shard_map/all_gather | solution.py:75
Sparse Core Ops, SparseCore 0:
  12.1 84.7 all-gather.1
where the time goes:
time: 253 us; the launch traced here: 252 us
  waiting for transfers between devices  80.3 us (32%)
  matrix products  63 us (25%)
  blocking collectives  56.7 us (22%)
  other arithmetic  33.5 us (13%)
  between operations  14.8 us (6%)
  local copies, waits for them, and re-layouts  4.07 us (2%)
    all_gather x1, waiting for transfers between devices, on_device(): lax.all_gather(normed, 'voc', axis=0, tiled=True)  80.3 us
    dot_general x1, matrix products, row_stats(): logits = jnp.dot(piece, weights, preferred_element_type=jnp.float32)  63 us
    psum x1, blocking collectives, on_device(): lax.psum((stats[1] * factor, stats[2] * factor, stats[3]), 'voc')  26 us
    reduce_sum x1, other arithmetic, row_stats(): total = jnp.sum(expo, axis=1)  23.9 us
    pmax x1, blocking collectives, on_device(): top = lax.pmax(stats[0], 'voc')  14.3 us
    all_gather x1, blocking collectives, on_device(): lax.all_gather(own_ent, 'tok', axis=0, tiled=True)  8.35 us
    all_gather x1, blocking collectives, on_device(): lax.all_gather(own_lp, 'tok', axis=0, tiled=True)  8.14 us
  transfers between devices with their start and end apart: 1, of which 1 were waited for; matrix products, arithmetic and copies ran while one was open for 2% of the time, Pallas kernels for 0%

commit v1 on v0

v1 whole, which is shorter than its diff:
```python
import jax
import jax.numpy as jnp
from jax import lax
from jax.sharding import PartitionSpec as P

MAXLEN = 1024
CHUNKS = 4


def slot_rows(positions, lengths, perm):
    count = lengths.shape[0]
    ident = jnp.arange(count, dtype=jnp.int32)
    starts = jnp.cumsum(lengths) - lengths
    request = jnp.sum((positions[:, None] >= starts[None, :]).astype(jnp.int32), axis=1) - 1
    start_of = jnp.sum(jnp.where(ident[None, :] == request[:, None], starts[None, :], 0), axis=1)
    slot_of = jnp.sum(jnp.where(perm[None, :] == request[:, None], ident[None, :], 0), axis=1)
    return slot_of * MAXLEN + positions - start_of


def row_stats(piece, weights, wanted):
    logits = jnp.dot(piece, weights, preferred_element_type=jnp.float32)
    top = jnp.max(logits, axis=1)
    expo = jnp.exp(logits - top[:, None])
    total = jnp.sum(expo, axis=1)
    moment = jnp.sum(expo * logits, axis=1)
    columns = jnp.arange(logits.shape[1], dtype=jnp.int32)
    picked = jnp.sum(jnp.where(columns[None, :] == wanted[:, None], logits, 0.0), axis=1)
    return jnp.stack([top, total, moment, picked], axis=0)


def on_device(hidden, gain, head, targets, lengths, perm):
    values = hidden.astype(jnp.float32)
    scale = lax.rsqrt(jnp.mean(values * values, axis=1, keepdims=True) + 1e-06)
    normed = (values * scale * gain.astype(jnp.float32)[None, :]).astype(jnp.bfloat16)
    n_tok = lax.axis_size("tok")
    n_voc = lax.axis_size("voc")
    local = normed.shape[0]
    group_rows = local * n_voc
    shard_cols = head.shape[1]
    col_base = lax.axis_index("voc") * shard_cols
    tok_index = lax.axis_index("tok")
    chunks = CHUNKS if local % (CHUNKS * 8) == 0 else 1
    step = local // chunks
    wanted = lax.dynamic_slice_in_dim(targets, tok_index * group_rows, group_rows, 0) - col_base
    wanted = wanted.reshape(n_voc, chunks, step)
    parts = []
    for j in range(chunks):
        piece = lax.all_gather(normed[j * step:(j + 1) * step], "voc", axis=0, tiled=True)
        parts.append(row_stats(piece, head, wanted[:, j, :].reshape(-1)).reshape(4, n_voc, step))
    stats = jnp.stack(parts, axis=2).reshape(4, group_rows)
    every = lax.all_gather(stats, "voc", axis=0)
    top = jnp.max(every[:, 0], axis=0)
    factor = jnp.exp(every[:, 0] - top[None, :])
    total = jnp.sum(every[:, 1] * factor, axis=0)
    moment = jnp.sum(every[:, 2] * factor, axis=0)
    picked = jnp.sum(every[:, 3], axis=0)
    lse = top + jnp.log(total)
    own = jnp.stack([picked - lse, lse - moment / total], axis=0)
    both = lax.all_gather(own, "tok", axis=1, tiled=True)
    out_rows = targets.shape[0] * 5 // 8 // (n_tok * n_voc)
    device = lax.axis_index(("tok", "voc"))
    positions = device * out_rows + jnp.arange(out_rows, dtype=jnp.int32)
    rows = slot_rows(positions, lengths, perm)
    return (both[0][rows], both[1][rows])


def solution(mesh):
    in_specs = (P(("tok", "voc"), None), P(), P(None, "voc"), P(), P(), P())
    out_specs = (P(("tok", "voc")), P(("tok", "voc")))
    return jax.shard_map(
        on_device, mesh=mesh, in_specs=in_specs, out_specs=out_specs, check_vma=False
    )
```

time: 253 us -> 197 us (0.78)
  waiting for transfers between devices: 80.3 us -> 34.6 us
  blocking collectives: 56.7 us -> 22.4 us
  matrix products: 63 us -> 81.6 us
  other arithmetic: 33.5 us -> 36.4 us
  local copies, waits for them, and re-layouts: 4.07 us -> 6.94 us
    all_gather x1 -> x4, waiting for transfers between devices: 80.3 us -> 32.7 us  [on_device(): lax.all_gather(normed[j * step:(j + 1) * step], 'voc', axis=0, tiled=True)]
    psum x1 -> x0, blocking collectives: 26 us -> none  [on_device(): lax.psum((stats[1] * factor, stats[2] * factor, stats[3]), 'voc')]
    dot_general x1 -> x4, matrix products: 63 us -> 81.6 us  [row_stats(): logits = jnp.dot(piece, weights, preferred_element_type=jnp.float32)]
    pmax x1 -> x0, blocking collectives: 14.3 us -> none  [on_device(): top = lax.pmax(stats[0], 'voc')]
    all_gather x2, blocking collectives: 16.5 us -> 22.4 us  [the longest x1 14.2 us: on_device(): every = lax.all_gather(stats, 'voc', axis=0)]
    reduce_sum x1 -> x4, other arithmetic: 23.9 us -> 29.2 us  [row_stats(): total = jnp.sum(expo, axis=1)]
  transfers between devices with their start and end apart: 1 -> 4, of which waited for: 1 -> 4; matrix products, arithmetic and copies ran while one was open for 2% -> 45% of each run, Pallas kernels for 0% -> 0%
where the time goes in v1:
time: 197 us; the launch traced here: 196 us
  matrix products  81.6 us (41%)
  other arithmetic  36.4 us (18%)
  waiting for transfers between devices  34.6 us (18%)
  blocking collectives  22.4 us (11%)
  between operations  13.9 us (7%)
  local copies, waits for them, and re-layouts  6.94 us (4%)
    dot_general x4, matrix products, row_stats(): logits = jnp.dot(piece, weights, preferred_element_type=jnp.float32)  81.6 us
    all_gather x4, waiting for transfers between devices, on_device(): lax.all_gather(normed[j * step:(j + 1) * step], 'voc', axis=0, tiled=True)  32.7 us
    reduce_sum x4, other arithmetic, row_stats(): total = jnp.sum(expo, axis=1)  29.2 us
    all_gather x1, blocking collectives, on_device(): every = lax.all_gather(stats, 'voc', axis=0)  14.2 us
    all_gather x1, blocking collectives, on_device(): both = lax.all_gather(own, 'tok', axis=1, tiled=True)  8.19 us
    gather x2, local copies, waits for them, and re-layouts, on_device(): return (both[0][rows], both[1][rows])  4.05 us
  transfers between devices with their start and end apart: 4, of which 4 were waited for; matrix products, arithmetic and copies ran while one was open for 45% of the time, Pallas kernels for 0%

profile of v1, /device:TPU:0, one launch (start us, length us, event | category | flops | bytes accessed | tf_op | source)
XLA Modules:
  0.0 196.0 jit_solution(17991150181426423881)
XLA Ops:
  7.2 0.7 convert_element_type.13
  7.9 1.5 fusion.4
  9.4 1.5 fusion.6
  11.0 1.0 fusion.13
  12.0 0.7 all-gather.9.cloned.1.call-update
  12.8 0.7 all-gather.7.cloned.1.call-update
  13.5 0.5 all-gather.5.cloned.1.call-update
  14.0 0.7 dynamic-slice_subtract_fusion
  14.8 0.1 reshape.169
  15.2 0.8 reduce-window.9
  16.0 0.7 bitcast_subtract_fusion
  16.7 0.1 convert_reduce_fusion
  16.8 0.7 select_reduce_fusion.5
  17.6 26.4 %all-gather.11.cloned.1.call-done = bf16[512,2048]{1,0:T(8,128)(2,1)} async-done(((bf16[64,2048]{1,0:T(8,128)(2,1)}), bf16[512,2048]{1,0:T(8,128)(2,1)}) %all-gather.11.cloned.1.call-update) | async-done | bytes 2097168 | tf_op jit(solution)/shard_map/all_gather | solution.py:48
  44.0 20.4 %fusion.16 = (f32[512]{0:T(512)S(1)}, f32[512,6288]{0,1:T(8,128)}) fusion(bf16[512,2048]{1,0:T(8,128)(2,1)} %all-gather.11.cloned.1.call-done, bf16[2048,6288]{0,1:T(8,128)(2,1)} %param.8), kind=kOutput, calls=%fused_computation.61 | convolution fusion | flops 13190111232 | bytes 40732672 | tf_op jit(solution)/shard_map/dot_general | solution.py:21
  64.4 7.3 %fusion = (f32[512]{0:T(512)S(1)}, f32[512]{0:T(512)S(1)}, f32[512]{0:T(512)S(1)}) fusion(f32[512,6288]{0,1:T(8,128)} %get-tuple-element.38, f32[512]{0:T(512)S(1)} %get-tuple-element.37, s32[512]{0:T(512)S(1)} %eq.95), kind=kLoop, calls=%fused_computation.6 | loop fusion | flops 22534656 | bytes 12888064 | tf_op jit(solution)/shard_map/reduce_sum | solution.py:24
  71.7 2.5 %all-gather.9.cloned.1.call-done = bf16[512,2048]{1,0:T(8,128)(2,1)} async-done(((bf16[64,2048]{1,0:T(8,128)(2,1)}), bf16[512,2048]{1,0:T(8,128)(2,1)}) %all-gather.9.cloned.1.call-update) | async-done | bytes 2097168 | tf_op jit(solution)/shard_map/all_gather | solution.py:48
  74.2 20.4 %fusion.17 = (f32[512]{0:T(512)S(1)}, f32[512,6288]{0,1:T(8,128)}) fusion(bf16[512,2048]{1,0:T(8,128)(2,1)} %all-gather.9.cloned.1.call-done, bf16[2048,6288]{0,1:T(8,128)(2,1)} %param.8), kind=kOutput, calls=%fused_computation.62 | convolution fusion | flops 13190111232 | bytes 40732672 | tf_op jit(solution)/shard_map/dot_general | solution.py:21
  94.6 7.3 %fusion.1 = (f32[512]{0:T(512)S(1)}, f32[512]{0:T(512)S(1)}, f32[512]{0:T(512)S(1)}) fusion(f32[512,6288]{0,1:T(8,128)} %get-tuple-element.40, f32[512]{0:T(512)S(1)} %get-tuple-element.39, s32[512]{0:T(512)S(1)} %eq.91), kind=kLoop, calls=%fused_computation.11 | loop fusion | flops 22534656 | bytes 12888064 | tf_op jit(solution)/shard_map/reduce_sum | solution.py:24
  101.9 0.1 stack.83
  102.0 0.1 stack.78
  102.1 0.1 stack.86
  102.1 0.1 stack.85
  102.2 0.1 stack.84
  102.3 0.1 stack.81
  102.4 0.1 stack.80
  102.5 0.1 stack.79
  102.6 1.8 all-gather.7.cloned.1.call-done
  104.4 20.4 %fusion.18 = (f32[512]{0:T(512)S(1)}, f32[512,6288]{0,1:T(8,128)}) fusion(bf16[512,2048]{1,0:T(8,128)(2,1)} %all-gather.7.cloned.1.call-done, bf16[2048,6288]{0,1:T(8,128)(2,1)} %param.8), kind=kOutput, calls=%fused_computation.63 | convolution fusion | flops 13190111232 | bytes 40732672 | tf_op jit(solution)/shard_map/dot_general | solution.py:21
  124.8 0.1 stack.73
  124.8 7.3 %fusion.2 = (f32[512]{0:T(512)S(1)}, f32[512]{0:T(512)S(1)}, f32[512]{0:T(512)S(1)}) fusion(f32[512,6288]{0,1:T(8,128)} %get-tuple-element.42, f32[512]{0:T(512)S(1)} %get-tuple-element.41, s32[512]{0:T(512)S(1)} %eq.87), kind=kLoop, calls=%fused_computation.16 | loop fusion | flops 22534656 | bytes 12888064 | tf_op jit(solution)/shard_map/reduce_sum | solution.py:24
  132.2 0.1 stack.76
  132.2 0.1 stack.75
  132.3 0.1 stack.74
  132.4 2.0 %all-gather.5.cloned.1.call-done = bf16[512,2048]{1,0:T(8,128)(2,1)} async-done(((bf16[64,2048]{1,0:T(8,128)(2,1)}), bf16[512,2048]{1,0:T(8,128)(2,1)}) %all-gather.5.cloned.1.call-update) | async-done | bytes 2097168 | tf_op jit(solution)/shard_map/all_gather | solution.py:48
  134.4 20.4 %fusion.19 = (f32[512]{0:T(512)S(1)}, f32[512,6288]{0,1:T(8,128)}) fusion(bf16[512,2048]{1,0:T(8,128)(2,1)} %all-gather.5.cloned.1.call-done, bf16[2048,6288]{0,1:T(8,128)(2,1)} %param.8), kind=kOutput, calls=%fused_computation.64 | convolution fusion | flops 13190111232 | bytes 40732672 | tf_op jit(solution)/shard_map/dot_general | solution.py:21
  154.8 0.1 stack.68
  154.9 7.2 %fusion.3 = (f32[512]{0:T(512)S(1)}, f32[512]{0:T(512)S(1)}, f32[512]{0:T(512)S(1)}) fusion(f32[512,6288]{0,1:T(8,128)} %get-tuple-element.44, f32[512]{0:T(512)S(1)} %get-tuple-element.43, s32[512]{0:T(512)S(1)} %eq.41), kind=kLoop, calls=%fused_computation.21 | loop fusion | flops 22534656 | bytes 12888064 | tf_op jit(solution)/shard_map/reduce_sum | solution.py:24
  162.1 0.1 stack.71
  162.2 0.1 stack.70
  162.3 0.1 stack.69
  162.5 0.1 all_gather_reshape.3
  162.6 14.2 %all_gather.22 = f32[8,4,2048]{2,1,0:T(4,128)S(1)} all-gather(f32[1,4,2048]{2,1,0:T(4,128)S(1)} %all_gather_reshape.3), channel_id=1, replica_groups=mesh['tok'=4,'voc'=8] {'voc'}, dimensions={0}, use_global_device_ids=true | all-gather | bytes 294912 | tf_op jit(solution)/shard_map/all_gather | solution.py:51
  176.8 0.2 fusion.14
  177.0 0.1 fusion.8
  177.2 8.2 %all_gather.23 = f32[2,8192]{1,0:T(2,128)S(1)} all-gather(f32[2,2048]{1,0:T(2,128)S(1)} %pad_maximum_fusion), channel_id=1, replica_groups=mesh['tok'=4,'voc'=8] {'tok'}, dimensions={1}, use_global_device_ids=true | all-gather | bytes 81920 | tf_op jit(solution)/shard_map/all_gather | solution.py:59
  185.4 2.0 %gather_fusion = f32[160]{0:T(256)} fusion(f32[8192]{0:T(1024)S(1)} %bitcast.39, s32[1024]{0:T(1024)S(1)} %pad_clamp_fusion), kind=kCustom, calls=%fused_computation | custom fusion | bytes 1920 | tf_op jit(solution)/shard_map/gather | solution.py:64
  187.4 2.0 %gather_fusion.1 = f32[160]{0:T(256)} fusion(f32[8192]{0:T(1024)S(1)} %bitcast.38, s32[1024]{0:T(1024)S(1)} %pad_clamp_fusion), kind=kCustom, calls=%fused_computation.1 | custom fusion | bytes 1920 | tf_op jit(solution)/shard_map/gather | solution.py:64
  (20 shorter events, 0.7 us)
Async XLA Ops:
  7.2 36.8 %all-gather.11.cloned.1.call-start = ((), (), s32[]{:S(2)}) async-start(), calls=%async_computation.3 | async-start | bytes 2359296 | tf_op jit(solution)/shard_map/all_gather | solution.py:48
  12.0 62.2 %all-gather.9.cloned.1.call-start = ((), (), s32[]{:S(2)}) async-start(), calls=%async_computation.2 | async-start | bytes 2359296 | tf_op jit(solution)/shard_map/all_gather | solution.py:48
  12.7 91.6 %all-gather.7.cloned.1.call-start = ((), (), s32[]{:S(2)}) async-start(), calls=%async_computation.1 | async-start | bytes 2359296 | tf_op jit(solution)/shard_map/all_gather | solution.py:48
  13.5 120.9 %all-gather.5.cloned.1.call-start = ((), (), s32[]{:S(2)}) async-start(), calls=%async_computation | async-start | bytes 2359296 | tf_op jit(solution)/shard_map/all_gather | solution.py:48
Sparse Core Ops, SparseCore 0:
  12.1 31.8 all-gather.10
  45.6 28.5 all-gather.8
  75.8 28.5 all-gather.6
  105.8 28.5 all-gather.4

commit v2 on v1

--- a/solution.py
+++ b/solution.py
@@ -2,9 +2,13 @@
 import jax.numpy as jnp
 from jax import lax
 from jax.sharding import PartitionSpec as P
+from jax.experimental import pallas as pl
+from jax.experimental.pallas import tpu as pltpu
 
 MAXLEN = 1024
-CHUNKS = 4
+CHUNKS = 2
+TILE_N = 512
+NEG = -1e30
 
 
 def slot_rows(positions, lengths, perm):
@@ -17,15 +21,66 @@
     return slot_of * MAXLEN + positions - start_of
 
 
+def stats_kernel(ncols, x_ref, w_ref, t_ref, m_out, s_out, e_out, p_out, m_sc, s_sc, e_sc, p_sc):
+    j = pl.program_id(1)
+    tn = w_ref.shape[1]
+
+    @pl.when(j == 0)
+    def _():
+        m_sc[...] = jnp.full(m_sc.shape, NEG, jnp.float32)
+        s_sc[...] = jnp.zeros(s_sc.shape, jnp.float32)
+        e_sc[...] = jnp.zeros(e_sc.shape, jnp.float32)
+        p_sc[...] = jnp.zeros(p_sc.shape, jnp.float32)
+
+    logits = jnp.dot(x_ref[...], w_ref[...], preferred_element_type=jnp.float32)
+    cols = j * tn + lax.broadcasted_iota(jnp.int32, logits.shape, 1)
+    logits = jnp.where(cols < ncols, logits, NEG)
+    old = m_sc[...]
+    new = jnp.maximum(old, jnp.max(logits, axis=1, keepdims=True))
+    alpha = jnp.exp(old - new)
+    expo = jnp.exp(logits - new)
+    s_sc[...] = s_sc[...] * alpha + jnp.sum(expo, axis=1, keepdims=True)
+    e_sc[...] = e_sc[...] * alpha + jnp.sum(expo * logits, axis=1, keepdims=True)
+    p_sc[...] = p_sc[...] + jnp.sum(jnp.where(cols == t_ref[...], logits, 0.0), axis=1, keepdims=True)
+    m_sc[...] = new
+
+    @pl.when(j == pl.num_programs(1) - 1)
+    def _():
+        m_out[...] = m_sc[...]
+        s_out[...] = s_sc[...]
+        e_out[...] = e_sc[...]
+        p_out[...] = p_sc[...]
+
+
 def row_stats(piece, weights, wanted):
-    logits = jnp.dot(piece, weights, preferred_element_type=jnp.float32)
-    top = jnp.max(logits, axis=1)
-    expo = jnp.exp(logits - top[:, None])
-    total = jnp.sum(expo, axis=1)
-    moment = jnp.sum(expo * logits, axis=1)
-    columns = jnp.arange(logits.shape[1], dtype=jnp.int32)
-    picked = jnp.sum(jnp.where(columns[None, :] == wanted[:, None], logits, 0.0), axis=1)
-    return jnp.stack([top, total, moment, picked], axis=0)
+    rows, depth = piece.shape
+    ncols = weights.shape[1]
+    tm = min(512, rows)
+    tn = TILE_N
+    grid = (rows // tm, pl.cdiv(ncols, tn))
+    wanted = jnp.where((wanted >= 0) & (wanted < ncols), wanted, -1).reshape(rows, 1)
+    row_spec = pl.BlockSpec((tm, 1), lambda i, j: (i, 0))
+    outs = pl.pallas_call(
+        lambda *refs: stats_kernel(ncols, *refs),
+        grid=grid,
+        in_specs=[
+            pl.BlockSpec((tm, depth), lambda i, j: (i, 0)),
+            pl.BlockSpec((depth, tn), lambda i, j: (0, j)),
+            row_spec,
+        ],
+        out_specs=[row_spec] * 4,
+        out_shape=[jax.ShapeDtypeStruct((rows, 1), jnp.float32)] * 4,
+        scratch_shapes=[pltpu.VMEM((tm, 1), jnp.float32)] * 4,
+        compiler_params=pltpu.CompilerParams(
+            dimension_semantics=("arbitrary", "arbitrary"), vmem_limit_bytes=48 * 1024 * 1024
+        ),
+        cost_estimate=pl.CostEstimate(
+            flops=2 * rows * depth * ncols,
+            transcendentals=rows * ncols,
+            bytes_accessed=2 * depth * ncols * (rows // tm) + 2 * rows * depth,
+        ),
+    )(piece, weights, wanted)
+    return jnp.stack([o.reshape(rows) for o in outs], axis=0)
 
 
 def on_device(hidden, gain, head, targets, lengths, perm):

time: 197 us -> 224 us (1.14)
  Pallas kernels: 0 us -> 125 us
  matrix products: 81.6 us -> 0 us
  local copies, waits for them, and re-layouts: 6.94 us -> 37 us
  other arithmetic: 36.4 us -> 7 us
  waiting for transfers between devices: 34.6 us -> 16.7 us
    pallas_call x0 -> x2, Pallas kernels: none -> 125 us  [row_stats(): pl.pallas_call(lambda *refs: stats_kernel(ncols, *refs), grid=grid, in_sp...]
    dot_general x4 -> x0, matrix products: 81.6 us -> none  [row_stats(): logits = jnp.dot(piece, weights, preferred_element_type=jnp.float32)]
    unnamed x0 -> x5, local copies, waits for them, and re-layouts: none -> 31.3 us
    reduce_sum x4 -> x0, other arithmetic: 29.2 us -> none  [row_stats(): total = jnp.sum(expo, axis=1)]
    all_gather x4 -> x2, waiting for transfers between devices: 32.7 us -> 15.9 us  [on_device(): lax.all_gather(normed[j * step:(j + 1) * step], 'voc', axis=0, tiled=True)]
  transfers between devices with their start and end apart: 4 -> 2, of which waited for: 4 -> 1; matrix products, arithmetic and copies ran while one was open for 45% -> 15% of each run, Pallas kernels for 0% -> 28%
where the time goes in v2:
time: 224 us; the launch traced here: 223 us
  Pallas kernels  125 us (56%)
  local copies, waits for them, and re-layouts  37 us (17%)
  blocking collectives  22.4 us (10%)
  waiting for transfers between devices  16.7 us (7%)
  between operations  14.2 us (6%)
  other arithmetic  7 us (3%)
    pallas_call x2, Pallas kernels, row_stats(): pl.pallas_call(lambda *refs: stats_kernel(ncols, *refs), grid=grid, in_sp...  125 us
    unnamed x5, local copies, waits for them, and re-layouts  31.3 us
    all_gather x2, waiting for transfers between devices, on_device(): lax.all_gather(normed[j * step:(j + 1) * step], 'voc', axis=0, tiled=True)  15.9 us
    all_gather x1, blocking collectives, on_device(): every = lax.all_gather(stats, 'voc', axis=0)  14.2 us
    all_gather x1, blocking collectives, on_device(): both = lax.all_gather(own, 'tok', axis=1, tiled=True)  8.19 us
  transfers between devices with their start and end apart: 2, of which 1 were waited for; matrix products, arithmetic and copies ran while one was open for 15% of the time, Pallas kernels for 28%

profile of v2, /device:TPU:0, one launch (start us, length us, event | category | flops | bytes accessed | tf_op | source)
XLA Modules:
  0.0 222.8 jit_solution(8315039672097503390)
XLA Ops:
  7.2 0.0 all-gather.3.cloned.1.call-start
  7.2 0.7 convert_element_type.13
  7.9 1.5 fusion
  9.4 1.5 fusion.2
  11.0 1.1 fusion.9
  12.1 0.0 all-gather.3.cloned.1.call-update
  12.1 0.0 all-gather.5.cloned.1.call-start
  12.1 0.7 all-gather.5.cloned.1.call-update
  12.8 0.7 dynamic-slice_subtract_fusion
  13.6 0.2 copy.34
  13.8 0.0 copy-start.1
  13.8 0.0 copy-start
  13.8 31.3 %copy.37.refs_1_ = bf16[2048,6288]{1,0:T(8,128)(2,1)} copy(bf16[2048,6288]{0,1:T(8,128)(2,1)} %param.8) | data formatting | bytes 51511296 | tf_op args[2]
  45.1 0.2 copy.38
  45.3 0.0 copy-done.1
  45.3 0.2 reduce-window.9
  45.5 0.1 convert_reduce_fusion
  45.6 0.0 copy-done
  45.6 0.1 select_reduce_fusion.1
  45.8 0.1 and_select_fusion.1.refs_2_
  45.8 0.1 and_select_fusion.refs_2_
  45.9 15.9 %all-gather.3.cloned.1.call-done.refs_0_ = bf16[1024,2048]{1,0:T(8,128)(2,1)} async-done(((bf16[128,2048]{1,0:T(8,128)(2,1)}), bf16[1024,2048]{1,0:T(8,128)(2,1)}) %all-gather.3.cloned.1.call-update) | async-done | bytes 4194320 | tf_op jit(solution)/shard_map/all_gather | solution.py:103
  61.8 62.7 %shard_map.77 = (f32[1024,1]{1,0:T(8,128)S(1)}, f32[1024,1]{1,0:T(8,128)S(1)}, f32[1024,1]{1,0:T(8,128)S(1)}, f32[1024,1]{1,0:T(8,128)S(1)}) custom-call(bf16[1024,2048]{1,0:T(8,128)(2,1)} %all-gather.3.cloned.1.call-done.refs_0_, bf16[2048,6288]{1,0:T(8,128)(2,1)} %copy.37.refs_1_, s32[1024,1]{1,0:T(8,128)S(1)} %and_select_fusion.1.refs_2_), custom_call_target="tpu_custom_call" | custom-call | flops 26373783552 | bytes 55705600 | tf_op jit(solution)/shard_map/pallas_call | solution.py:63
  124.6 0.2 reduce.2
  124.8 0.2 reduce.3
  125.0 0.2 reduce.4
  125.2 0.2 reduce.5
  125.4 0.0 all-gather.5.cloned.1.call-done.refs_0_
  125.4 62.7 %shard_map.78 = (f32[1024,1]{1,0:T(8,128)S(1)}, f32[1024,1]{1,0:T(8,128)S(1)}, f32[1024,1]{1,0:T(8,128)S(1)}, f32[1024,1]{1,0:T(8,128)S(1)}) custom-call(bf16[1024,2048]{1,0:T(8,128)(2,1)} %all-gather.5.cloned.1.call-done.refs_0_, bf16[2048,6288]{1,0:T(8,128)(2,1)} %copy.37.refs_1_, s32[1024,1]{1,0:T(8,128)S(1)} %and_select_fusion.refs_2_), custom_call_target="tpu_custom_call" | custom-call | flops 26373783552 | bytes 55705600 | tf_op jit(solution)/shard_map/pallas_call | solution.py:63
  188.2 0.2 reduce.6
  188.4 0.2 reduce.7
  188.6 0.2 reduce.8
  188.8 0.2 reduce.9
  189.1 14.2 %all_gather.14 = f32[8,4,2048]{2,1,0:T(4,128)S(1)} all-gather(f32[1,4,2048]{2,1,0:T(4,128)S(1)} %all_gather_reshape.3), channel_id=1, replica_groups=mesh['tok'=4,'voc'=8] {'voc'}, dimensions={0}, use_global_device_ids=true | all-gather | bytes 294912 | tf_op jit(solution)/shard_map/all_gather | solution.py:106
  203.3 0.2 fusion.10
  203.6 0.1 fusion.4
  203.7 8.2 %all_gather.15 = f32[2,8192]{1,0:T(2,128)S(1)} all-gather(f32[2,2048]{1,0:T(2,128)S(1)} %pad_maximum_fusion), channel_id=1, replica_groups=mesh['tok'=4,'voc'=8] {'tok'}, dimensions={1}, use_global_device_ids=true | all-gather | bytes 81920 | tf_op jit(solution)/shard_map/all_gather | solution.py:114
  211.9 0.1 fusion.11
  211.9 2.0 gather_fusion.1
  214.0 2.0 gather_fusion
  (13 shorter events, 0.1 us)
Async XLA Ops:
  7.2 54.7 %all-gather.3.cloned.1.call-start = ((), (), s32[]{:S(2)}) async-start(), calls=%async_computation | async-start | bytes 4718592 | tf_op jit(solution)/shard_map/all_gather | solution.py:103
  12.1 113.3 %all-gather.5.cloned.1.call-start = ((), (), s32[]{:S(2)}) async-start(), calls=%async_computation.1 | async-start | bytes 4718592 | tf_op jit(solution)/shard_map/all_gather | solution.py:103
  13.8 31.5 %copy-start.1 = (s32[8]{0:T(128)S(1)}, s32[8]{0:T(128)}, u32[]{:S(2)}) copy-start(s32[8]{0:T(128)} %param.10) | copy-start | bytes 100
  13.8 31.8 %copy-start = (s32[8]{0:T(128)S(1)}, s32[8]{0:T(128)}, u32[]{:S(2)}) copy-start(s32[8]{0:T(128)} %param.11) | copy-start | bytes 100
Sparse Core Ops, SparseCore 0:
  12.2 49.5 all-gather.2
  63.4 45.6 all-gather.4

commit v3 on v2

--- a/solution.py
+++ b/solution.py
@@ -21,9 +21,9 @@
     return slot_of * MAXLEN + positions - start_of
 
 
-def stats_kernel(ncols, x_ref, w_ref, t_ref, m_out, s_out, e_out, p_out, m_sc, s_sc, e_sc, p_sc):
+def stats_kernel(x_ref, w_ref, t_ref, m_out, s_out, e_out, p_out, m_sc, s_sc, e_sc, p_sc):
     j = pl.program_id(1)
-    tn = w_ref.shape[1]
+    tn = w_ref.shape[0]
 
     @pl.when(j == 0)
     def _():
@@ -32,16 +32,18 @@
         e_sc[...] = jnp.zeros(e_sc.shape, jnp.float32)
         p_sc[...] = jnp.zeros(p_sc.shape, jnp.float32)
 
-    logits = jnp.dot(x_ref[...], w_ref[...], preferred_element_type=jnp.float32)
-    cols = j * tn + lax.broadcasted_iota(jnp.int32, logits.shape, 1)
-    logits = jnp.where(cols < ncols, logits, NEG)
+    logits = lax.dot_general(
+        x_ref[...], w_ref[...], (((1,), (1,)), ((), ())), preferred_element_type=jnp.float32
+    )
     old = m_sc[...]
     new = jnp.maximum(old, jnp.max(logits, axis=1, keepdims=True))
     alpha = jnp.exp(old - new)
     expo = jnp.exp(logits - new)
     s_sc[...] = s_sc[...] * alpha + jnp.sum(expo, axis=1, keepdims=True)
     e_sc[...] = e_sc[...] * alpha + jnp.sum(expo * logits, axis=1, keepdims=True)
-    p_sc[...] = p_sc[...] + jnp.sum(jnp.where(cols == t_ref[...], logits, 0.0), axis=1, keepdims=True)
+    lanes = lax.broadcasted_iota(jnp.int32, logits.shape, 1)
+    hit = lanes == t_ref[...] - j * tn
+    p_sc[...] = p_sc[...] + jnp.sum(jnp.where(hit, logits, 0.0), axis=1, keepdims=True)
     m_sc[...] = new
 
     @pl.when(j == pl.num_programs(1) - 1)
@@ -52,20 +54,37 @@
         p_out[...] = p_sc[...]
 
 
-def row_stats(piece, weights, wanted):
+def dense_stats(piece, rows_t, wanted, base):
+    logits = lax.dot_general(piece, rows_t, (((1,), (1,)), ((), ())), preferred_element_type=jnp.float32)
+    top = jnp.max(logits, axis=1)
+    expo = jnp.exp(logits - top[:, None])
+    total = jnp.sum(expo, axis=1)
+    moment = jnp.sum(expo * logits, axis=1)
+    columns = base + jnp.arange(logits.shape[1], dtype=jnp.int32)
+    picked = jnp.sum(jnp.where(columns[None, :] == wanted[:, None], logits, 0.0), axis=1)
+    return top, total, moment, picked
+
+
+def merge(a, b):
+    top = jnp.maximum(a[0], b[0])
+    fa, fb = jnp.exp(a[0] - top), jnp.exp(b[0] - top)
+    return top, a[1] * fa + b[1] * fb, a[2] * fa + b[2] * fb, a[3] + b[3]
+
+
+def row_stats(piece, weights_t, wanted):
     rows, depth = piece.shape
-    ncols = weights.shape[1]
+    ncols = weights_t.shape[0]
     tm = min(512, rows)
     tn = TILE_N
-    grid = (rows // tm, pl.cdiv(ncols, tn))
-    wanted = jnp.where((wanted >= 0) & (wanted < ncols), wanted, -1).reshape(rows, 1)
+    full = ncols // tn
+    wanted = jnp.where((wanted >= 0) & (wanted < ncols), wanted, -1)
     row_spec = pl.BlockSpec((tm, 1), lambda i, j: (i, 0))
     outs = pl.pallas_call(
-        lambda *refs: stats_kernel(ncols, *refs),
-        grid=grid,
+        stats_kernel,
+        grid=(rows // tm, full),
         in_specs=[
             pl.BlockSpec((tm, depth), lambda i, j: (i, 0)),
-            pl.BlockSpec((depth, tn), lambda i, j: (0, j)),
+            pl.BlockSpec((tn, depth), lambda i, j: (j, 0)),
             row_spec,
         ],
         out_specs=[row_spec] * 4,
@@ -75,12 +94,15 @@
             dimension_semantics=("arbitrary", "arbitrary"), vmem_limit_bytes=48 * 1024 * 1024
         ),
         cost_estimate=pl.CostEstimate(
-            flops=2 * rows * depth * ncols,
-            transcendentals=rows * ncols,
-            bytes_accessed=2 * depth * ncols * (rows // tm) + 2 * rows * depth,
+            flops=2 * rows * depth * full * tn,
+            transcendentals=rows * full * tn,
+            bytes_accessed=2 * depth * full * tn * (rows // tm) + 2 * rows * depth,
         ),
-    )(piece, weights, wanted)
-    return jnp.stack([o.reshape(rows) for o in outs], axis=0)
+    )(piece, weights_t, wanted.reshape(rows, 1))
+    got = tuple(o.reshape(rows) for o in outs)
+    if full * tn < ncols:
+        got = merge(got, dense_stats(piece, weights_t[full * tn:], wanted, full * tn))
+    return jnp.stack(got, axis=0)
 
 
 def on_device(hidden, gain, head, targets, lengths, perm):
@@ -98,10 +120,11 @@
     step = local // chunks
     wanted = lax.dynamic_slice_in_dim(targets, tok_index * group_rows, group_rows, 0) - col_base
     wanted = wanted.reshape(n_voc, chunks, step)
+    head_t = head.T
     parts = []
     for j in range(chunks):
         piece = lax.all_gather(normed[j * step:(j + 1) * step], "voc", axis=0, tiled=True)
-        parts.append(row_stats(piece, head, wanted[:, j, :].reshape(-1)).reshape(4, n_voc, step))
+        parts.append(row_stats(piece, head_t, wanted[:, j, :].reshape(-1)).reshape(4, n_voc, step))
     stats = jnp.stack(parts, axis=2).reshape(4, group_rows)
     every = lax.all_gather(stats, "voc", axis=0)
     top = jnp.max(every[:, 0], axis=0)

time: 224 us -> 223 us (level)
  waiting for transfers between devices: 16.7 us -> 47.9 us
  local copies, waits for them, and re-layouts: 37 us -> 5.81 us
  Pallas kernels: 125 us -> 118 us
  matrix products: 0 us -> 6.67 us
    unnamed x5 -> x6, local copies, waits for them, and re-layouts: 31.3 us -> 0.01 us
    all_gather x2, waiting for transfers between devices: 15.9 us -> 47.2 us  [on_device(): lax.all_gather(normed[j * step:(j + 1) * step], 'voc', axis=0, tiled=True)]
    pallas_call x2, Pallas kernels: 125 us -> 118 us  [row_stats(): pl.pallas_call(stats_kernel, grid=(rows // tm, full), in_specs=[pl.BlockS...]
    dot_general x0 -> x2, matrix products: none -> 6.67 us  [dense_stats(): lax.dot_general(piece, rows_t, (((1,), (1,)), ((), ())), preferred_elemen...]
  transfers between devices with their start and end apart: 2 -> 2, of which waited for: 1 -> 1; matrix products, arithmetic and copies ran while one was open for 15% -> 1% of each run, Pallas kernels for 28% -> 26%
where the time goes in v3:
time: 223 us; the launch traced here: 222 us
  Pallas kernels  118 us (53%)
  waiting for transfers between devices  47.9 us (21%)
  blocking collectives  22.4 us (10%)
  between operations  14.3 us (6%)
  other arithmetic  7.44 us (3%)
  matrix products  6.67 us (3%)
  local copies, waits for them, and re-layouts  5.81 us (3%)
    pallas_call x2, Pallas kernels, row_stats(): pl.pallas_call(stats_kernel, grid=(rows // tm, full), in_specs=[pl.BlockS...  118 us
    all_gather x2, waiting for transfers between devices, on_device(): lax.all_gather(normed[j * step:(j + 1) * step], 'voc', axis=0, tiled=True)  47.2 us
    all_gather x1, blocking collectives, on_device(): every = lax.all_gather(stats, 'voc', axis=0)  14.2 us
    all_gather x1, blocking collectives, on_device(): both = lax.all_gather(own, 'tok', axis=1, tiled=True)  8.19 us
    dot_general x2, matrix products, dense_stats(): lax.dot_general(piece, rows_t, (((1,), (1,)), ((), ())), preferred_elemen...  6.67 us
  transfers between devices with their start and end apart: 2, of which 1 were waited for; matrix products, arithmetic and copies ran while one was open for 1% of the time, Pallas kernels for 26%

profile of v3, /device:TPU:0, one launch (start us, length us, event | category | flops | bytes accessed | tf_op | source)
XLA Modules:
  0.0 222.2 jit_solution(17963376404899619255)
XLA Ops:
  7.2 0.0 copy-start.2
  7.2 0.0 copy-start
  7.2 0.0 all-gather.5.cloned.1.call-start
  7.2 0.7 convert_element_type.13
  7.9 1.5 fusion
  9.4 1.5 fusion.2
  11.0 1.2 fusion.23
  12.2 0.0 all-gather.5.cloned.1.call-update
  12.2 0.0 all-gather.3.cloned.1.call-start
  12.2 0.7 all-gather.3.cloned.1.call-update
  12.9 0.7 dynamic-slice_subtract_fusion
  13.7 0.2 copy.31
  13.9 0.2 copy.28
  14.1 0.0 copy-done.2
  14.1 0.2 reduce-window.9
  14.3 0.1 convert_reduce_fusion
  14.4 0.0 copy-done
  14.4 0.1 select_reduce_fusion.3
  14.6 0.1 and_select_fusion.t_ref
  14.7 0.1 and_select_fusion.1.t_ref
  14.8 47.2 %all-gather.5.cloned.1.call-done.x_ref = bf16[1024,2048]{1,0:T(8,128)(2,1)} async-done(((bf16[128,2048]{1,0:T(8,128)(2,1)}), bf16[1024,2048]{1,0:T(8,128)(2,1)}) %all-gather.5.cloned.1.call-update) | async-done | bytes 4194320 | tf_op jit(solution)/shard_map/all_gather | solution.py:126
  61.9 58.8 %shard_map.78 = (f32[1024,1]{1,0:T(8,128)S(1)}, f32[1024,1]{1,0:T(8,128)S(1)}, f32[1024,1]{1,0:T(8,128)S(1)}, f32[1024,1]{1,0:T(8,128)S(1)}) custom-call(bf16[1024,2048]{1,0:T(8,128)(2,1)} %all-gather.5.cloned.1.call-done.x_ref, bf16[6288,2048]{1,0:T(8,128)(2,1)} %bitcast.142, s32[1024,1]{1,0:T(8,128)S(1)} %and_select_fusion.t_ref), custom_call_target="tpu_custom_call" | custom-call | flops 25769803776 | bytes 54525952 | tf_op jit(solution)/shard_map/pallas_call | solution.py:82
  120.7 0.2 reduce.6
  120.9 0.2 reduce.8
  121.2 0.2 reduce.7
  121.4 0.2 reduce.9
  121.6 0.0 all-gather.3.cloned.1.call-done.x_ref
  121.6 58.8 %shard_map.77 = (f32[1024,1]{1,0:T(8,128)S(1)}, f32[1024,1]{1,0:T(8,128)S(1)}, f32[1024,1]{1,0:T(8,128)S(1)}, f32[1024,1]{1,0:T(8,128)S(1)}) custom-call(bf16[1024,2048]{1,0:T(8,128)(2,1)} %all-gather.3.cloned.1.call-done.x_ref, bf16[6288,2048]{1,0:T(8,128)(2,1)} %bitcast.143, s32[1024,1]{1,0:T(8,128)S(1)} %and_select_fusion.1.t_ref), custom_call_target="tpu_custom_call" | custom-call | flops 25769803776 | bytes 54525952 | tf_op jit(solution)/shard_map/pallas_call | solution.py:82
  180.4 0.2 reduce.2
  180.7 0.2 reduce.4
  180.9 0.2 reduce.3
  181.1 0.2 reduce.5
  181.3 0.0 copy-start.1
  181.3 4.0 %fusion.28 = (f32[1024]{0:T(1024)S(1)}, f32[1024,144]{0,1:T(8,128)S(1)}) fusion(bf16[1024,2048]{1,0:T(8,128)(2,1)} %all-gather.5.cloned.1.call-done.x_ref, bf16[6288,2048]{1,0:T(8,128)(2,1)} %bitcast.144), kind=kOutput, calls=%fused_computation.82 | convolution fusion | flops 604126208 | bytes 5378048 | tf_op jit(solution)/shard_map/dot_general | solution.py:58
  185.3 0.0 copy-done.1
  185.3 2.7 %fusion.27 = (f32[1024]{0:T(1024)S(1)}, f32[1024,144]{0,1:T(8,128)S(1)}) fusion(bf16[1024,2048]{1,0:T(8,128)(2,1)S(1)} %copy-done.1, bf16[6288,2048]{1,0:T(8,128)(2,1)} %bitcast.145), kind=kOutput, calls=%fused_computation.81 | convolution fusion | flops 604126208 | bytes 5378048 | tf_op jit(solution)/shard_map/dot_general | solution.py:58
  188.0 0.4 fusion.4
  188.5 14.2 %all_gather.14 = f32[8,4,2048]{2,1,0:T(4,128)S(1)} all-gather(f32[1,4,2048]{2,1,0:T(4,128)S(1)} %all_gather_reshape.3), channel_id=1, replica_groups=mesh['tok'=4,'voc'=8] {'voc'}, dimensions={0}, use_global_device_ids=true | all-gather | bytes 294912 | tf_op jit(solution)/shard_map/all_gather | solution.py:129
  202.7 0.2 fusion.24
  203.0 0.1 fusion.10
  203.1 8.2 %all_gather.15 = f32[2,8192]{1,0:T(2,128)S(1)} all-gather(f32[2,2048]{1,0:T(2,128)S(1)} %pad_maximum_fusion), channel_id=1, replica_groups=mesh['tok'=4,'voc'=8] {'tok'}, dimensions={1}, use_global_device_ids=true | all-gather | bytes 81920 | tf_op jit(solution)/shard_map/all_gather | solution.py:137
  211.3 0.1 fusion.25
  211.4 2.0 gather_fusion
  213.4 2.0 gather_fusion.1
  (18 shorter events, 0.2 us)
Async XLA Ops:
  7.2 7.0 %copy-start.2 = (s32[8]{0:T(128)S(1)}, s32[8]{0:T(128)}, u32[]{:S(2)}) copy-start(s32[8]{0:T(128)} %param.10) | copy-start | bytes 100
  7.2 7.3 %copy-start = (s32[8]{0:T(128)S(1)}, s32[8]{0:T(128)}, u32[]{:S(2)}) copy-start(s32[8]{0:T(128)} %param.11) | copy-start | bytes 100
  7.2 54.7 %all-gather.5.cloned.1.call-start = ((), (), s32[]{:S(2)}) async-start(), calls=%async_computation.1 | async-start | bytes 4718592 | tf_op jit(solution)/shard_map/all_gather | solution.py:126
  12.2 109.4 %all-gather.3.cloned.1.call-start = ((), (), s32[]{:S(2)}) async-start(), calls=%async_computation | async-start | bytes 4718592 | tf_op jit(solution)/shard_map/all_gather | solution.py:126
  181.3 4.0 %copy-start.1 = (bf16[1024,2048]{1,0:T(8,128)(2,1)S(1)}, bf16[1024,2048]{1,0:T(8,128)(2,1)}, u32[]{:S(2)}) copy-start(bf16[1024,2048]{1,0:T(8,128)(2,1)} %all-gather.3.cloned.1.call-done.x_ref) | copy-start | bytes 12582916
Sparse Core Ops, SparseCore 0:
  12.3 49.5 all-gather.4
  63.5 45.6 all-gather.2

commit v4 on v3

--- a/solution.py
+++ b/solution.py
@@ -24,6 +24,7 @@
 def stats_kernel(x_ref, w_ref, t_ref, m_out, s_out, e_out, p_out, m_sc, s_sc, e_sc, p_sc):
     j = pl.program_id(1)
     tn = w_ref.shape[0]
+    lane = m_sc.shape[1]
 
     @pl.when(j == 0)
     def _():
@@ -35,16 +36,27 @@
     logits = lax.dot_general(
         x_ref[...], w_ref[...], (((1,), (1,)), ((), ())), preferred_element_type=jnp.float32
     )
+    groups = [logits[:, k * lane:(k + 1) * lane] for k in range(tn // lane)]
+    top = groups[0]
+    for g in groups[1:]:
+        top = jnp.maximum(top, g)
     old = m_sc[...]
-    new = jnp.maximum(old, jnp.max(logits, axis=1, keepdims=True))
+    new = jnp.maximum(old, top)
     alpha = jnp.exp(old - new)
-    expo = jnp.exp(logits - new)
-    s_sc[...] = s_sc[...] * alpha + jnp.sum(expo, axis=1, keepdims=True)
-    e_sc[...] = e_sc[...] * alpha + jnp.sum(expo * logits, axis=1, keepdims=True)
-    lanes = lax.broadcasted_iota(jnp.int32, logits.shape, 1)
-    hit = lanes == t_ref[...] - j * tn
-    p_sc[...] = p_sc[...] + jnp.sum(jnp.where(hit, logits, 0.0), axis=1, keepdims=True)
+    total = s_sc[...] * alpha
+    moment = e_sc[...] * alpha
+    picked = p_sc[...]
+    shift = t_ref[...] - j * tn
+    lanes = lax.broadcasted_iota(jnp.int32, top.shape, 1)
+    for k, g in enumerate(groups):
+        expo = jnp.exp(g - new)
+        total = total + expo
+        moment = moment + expo * g
+        picked = picked + jnp.where(lanes == shift - k * lane, g, 0.0)
     m_sc[...] = new
+    s_sc[...] = total
+    e_sc[...] = moment
+    p_sc[...] = picked
 
     @pl.when(j == pl.num_programs(1) - 1)
     def _():
@@ -76,32 +88,39 @@
     ncols = weights_t.shape[0]
     tm = min(512, rows)
     tn = TILE_N
+    lane = 128
     full = ncols // tn
     wanted = jnp.where((wanted >= 0) & (wanted < ncols), wanted, -1)
-    row_spec = pl.BlockSpec((tm, 1), lambda i, j: (i, 0))
-    outs = pl.pallas_call(
-        stats_kernel,
-        grid=(rows // tm, full),
-        in_specs=[
-            pl.BlockSpec((tm, depth), lambda i, j: (i, 0)),
-            pl.BlockSpec((tn, depth), lambda i, j: (j, 0)),
-            row_spec,
-        ],
-        out_specs=[row_spec] * 4,
-        out_shape=[jax.ShapeDtypeStruct((rows, 1), jnp.float32)] * 4,
-        scratch_shapes=[pltpu.VMEM((tm, 1), jnp.float32)] * 4,
-        compiler_params=pltpu.CompilerParams(
-            dimension_semantics=("arbitrary", "arbitrary"), vmem_limit_bytes=48 * 1024 * 1024
-        ),
-        cost_estimate=pl.CostEstimate(
-            flops=2 * rows * depth * full * tn,
-            transcendentals=rows * full * tn,
-            bytes_accessed=2 * depth * full * tn * (rows // tm) + 2 * rows * depth,
-        ),
-    )(piece, weights_t, wanted.reshape(rows, 1))
-    got = tuple(o.reshape(rows) for o in outs)
+    got = None
+    if full > 0:
+        row_spec = pl.BlockSpec((tm, lane), lambda i, j: (i, 0))
+        outs = pl.pallas_call(
+            stats_kernel,
+            grid=(rows // tm, full),
+            in_specs=[
+                pl.BlockSpec((tm, depth), lambda i, j: (i, 0)),
+                pl.BlockSpec((tn, depth), lambda i, j: (j, 0)),
+                row_spec,
+            ],
+            out_specs=[row_spec] * 4,
+            out_shape=[jax.ShapeDtypeStruct((rows, lane), jnp.float32)] * 4,
+            scratch_shapes=[pltpu.VMEM((tm, lane), jnp.float32)] * 4,
+            compiler_params=pltpu.CompilerParams(
+                dimension_semantics=("arbitrary", "arbitrary"), vmem_limit_bytes=48 * 1024 * 1024
+            ),
+            cost_estimate=pl.CostEstimate(
+                flops=2 * rows * depth * full * tn,
+                transcendentals=rows * full * tn,
+                bytes_accessed=2 * depth * full * tn * (rows // tm) + 2 * rows * depth,
+            ),
+        )(piece, weights_t, jnp.broadcast_to(wanted[:, None], (rows, lane)))
+        m, s, e, p = outs
+        top = jnp.max(m, axis=1)
+        scale = jnp.exp(m - top[:, None])
+        got = (top, jnp.sum(s * scale, axis=1), jnp.sum(e * scale, axis=1), jnp.sum(p, axis=1))
     if full * tn < ncols:
-        got = merge(got, dense_stats(piece, weights_t[full * tn:], wanted, full * tn))
+        rest = dense_stats(piece, weights_t[full * tn:], wanted, full * tn)
+        got = rest if got is None else merge(got, rest)
     return jnp.stack(got, axis=0)
 
 

time: 223 us -> 198 us (0.89)
  Pallas kernels: 118 us -> 83.4 us
  waiting for transfers between devices: 47.9 us -> 52.8 us
    pallas_call x2, Pallas kernels: 118 us -> 83.4 us  [row_stats(): pl.pallas_call(stats_kernel, grid=(rows // tm, full), in_specs=[pl.BlockS...]
    all_gather x2, waiting for transfers between devices: 47.2 us -> 52.1 us  [on_device(): lax.all_gather(normed[j * step:(j + 1) * step], 'voc', axis=0, tiled=True)]
    reduce_sum x0 -> x4, other arithmetic: none -> 3.49 us  [the longest x2 2.5 us: row_stats(): jnp.sum(p, axis=1)]
  transfers between devices with their start and end apart: 2 -> 2, of which waited for: 1 -> 2; matrix products, arithmetic and copies ran while one was open for 1% -> 1% of each run, Pallas kernels for 26% -> 21%
where the time goes in v4:
time: 198 us; the launch traced here: 197 us
  Pallas kernels  83.4 us (42%)
  waiting for transfers between devices  52.8 us (27%)
  blocking collectives  22.4 us (11%)
  between operations  14.3 us (7%)
  other arithmetic  9.6 us (5%)
  local copies, waits for them, and re-layouts  7.41 us (4%)
  matrix products  6.64 us (3%)
    pallas_call x2, Pallas kernels, row_stats(): pl.pallas_call(stats_kernel, grid=(rows // tm, full), in_specs=[pl.BlockS...  83.4 us
    all_gather x2, waiting for transfers between devices, on_device(): lax.all_gather(normed[j * step:(j + 1) * step], 'voc', axis=0, tiled=True)  52.1 us
    all_gather x1, blocking collectives, on_device(): every = lax.all_gather(stats, 'voc', axis=0)  14.2 us
    all_gather x1, blocking collectives, on_device(): both = lax.all_gather(own, 'tok', axis=1, tiled=True)  8.19 us
    dot_general x2, matrix products, dense_stats(): lax.dot_general(piece, rows_t, (((1,), (1,)), ((), ())), preferred_elemen...  6.64 us
    gather x2, local copies, waits for them, and re-layouts, on_device(): return (both[0][rows], both[1][rows])  4.05 us
  transfers between devices with their start and end apart: 2, of which 2 were waited for; matrix products, arithmetic and copies ran while one was open for 1% of the time, Pallas kernels for 21%

profile of v4, /device:TPU:0, one launch (start us, length us, event | category | flops | bytes accessed | tf_op | source)
XLA Modules:
  0.0 196.6 jit_solution(9959410149088731440)
XLA Ops:
  7.2 0.0 copy-start.4
  7.2 0.0 copy-start.2
  7.2 0.0 all-gather.3.cloned.1.call-start
  7.2 0.7 convert_element_type.13
  7.9 1.5 fusion
  9.4 1.5 fusion.2
  11.0 1.2 fusion.15
  12.2 0.0 all-gather.3.cloned.1.call-update
  12.2 0.0 all-gather.5.cloned.1.call-start
  12.2 0.7 all-gather.5.cloned.1.call-update
  12.9 0.0 copy-done.4
  13.0 0.2 reduce-window.9
  13.2 0.1 convert_reduce_fusion
  13.2 0.0 copy-done.2
  13.3 0.1 select_reduce_fusion.3
  13.4 0.7 dynamic-slice_subtract_fusion
  14.1 47.8 %all-gather.3.cloned.1.call-done.x_ref = bf16[1024,2048]{1,0:T(8,128)(2,1)} async-done(((bf16[128,2048]{1,0:T(8,128)(2,1)}), bf16[1024,2048]{1,0:T(8,128)(2,1)}) %all-gather.3.cloned.1.call-update) | async-done | bytes 4194320 | tf_op jit(solution)/shard_map/all_gather | solution.py:145
  61.9 0.2 broadcast_in_dim.29.t_ref
  62.1 41.8 %shard_map.77 = (f32[1024,128]{1,0:T(8,128)S(1)}, f32[1024,128]{1,0:T(8,128)S(1)}, f32[1024,128]{1,0:T(8,128)S(1)}, f32[1024,128]{1,0:T(8,128)S(1)}) custom-call(bf16[1024,2048]{1,0:T(8,128)(2,1)} %all-gather.3.cloned.1.call-done.x_ref, bf16[6288,2048]{1,0:T(8,128)(2,1)} %bitcast.108, s32[1024,128]{1,0:T(8,128)S(1)} %broadcast_in_dim.29.t_ref), custom_call_target="tpu_custom_call" | custom-call | flops 25769803776 | bytes 54525952 | tf_op jit(solution)/shard_map/pallas_call | solution.py:97
  103.9 0.0 copy-start
  103.9 0.9 copy-done
  104.8 0.2 reduce_max.53
  105.0 4.2 %all-gather.5.cloned.1.call-done.x_ref = bf16[1024,2048]{1,0:T(8,128)(2,1)} async-done(((bf16[128,2048]{1,0:T(8,128)(2,1)}), bf16[1024,2048]{1,0:T(8,128)(2,1)}) %all-gather.5.cloned.1.call-update) | async-done | bytes 4194320 | tf_op jit(solution)/shard_map/all_gather | solution.py:145
  109.2 0.2 broadcast_in_dim.31.t_ref
  109.4 41.6 %shard_map.78 = (f32[1024,128]{1,0:T(8,128)S(1)}, f32[1024,128]{1,0:T(8,128)S(1)}, f32[1024,128]{1,0:T(8,128)S(1)}, f32[1024,128]{1,0:T(8,128)S(1)}) custom-call(bf16[1024,2048]{1,0:T(8,128)(2,1)} %all-gather.5.cloned.1.call-done.x_ref, bf16[6288,2048]{1,0:T(8,128)(2,1)} %bitcast.109, s32[1024,128]{1,0:T(8,128)S(1)} %broadcast_in_dim.31.t_ref), custom_call_target="tpu_custom_call" | custom-call | flops 25769803776 | bytes 54525952 | tf_op jit(solution)/shard_map/pallas_call | solution.py:97
  151.1 0.0 copy-start.1
  151.1 0.8 copy-done.1
  151.9 0.2 reduce_max.57
  152.1 1.2 reduce_sum.198
  153.4 1.2 reduce_sum.208
  154.6 0.0 copy-start.3
  154.6 4.0 %fusion.19 = (f32[1024]{0:T(1024)S(1)}, f32[1024,144]{0,1:T(8,128)S(1)}) fusion(bf16[1024,2048]{1,0:T(8,128)(2,1)} %all-gather.3.cloned.1.call-done.x_ref, bf16[6288,2048]{1,0:T(8,128)(2,1)} %bitcast.110), kind=kOutput, calls=%fused_computation.67 | convolution fusion | flops 604126208 | bytes 5378048 | tf_op jit(solution)/shard_map/dot_general | solution.py:70
  158.7 0.0 copy-done.3
  158.7 2.6 %fusion.20 = (f32[1024]{0:T(1024)S(1)}, f32[1024,144]{0,1:T(8,128)S(1)}) fusion(bf16[1024,2048]{1,0:T(8,128)(2,1)S(1)} %copy-done.3, bf16[6288,2048]{1,0:T(8,128)(2,1)} %bitcast.111), kind=kOutput, calls=%fused_computation.68 | convolution fusion | flops 604126208 | bytes 5378048 | tf_op jit(solution)/shard_map/dot_general | solution.py:70
  161.3 0.4 fusion.4
  161.7 0.5 multiply_reduce_fusion.5
  162.2 0.5 multiply_reduce_fusion.3
  162.9 14.2 %all_gather.14 = f32[8,4,2048]{2,1,0:T(4,128)S(1)} all-gather(f32[1,4,2048]{2,1,0:T(4,128)S(1)} %all_gather_reshape.3), channel_id=1, replica_groups=mesh['tok'=4,'voc'=8] {'voc'}, dimensions={0}, use_global_device_ids=true | all-gather | bytes 294912 | tf_op jit(solution)/shard_map/all_gather | solution.py:148
  177.1 0.2 fusion.16
  177.3 0.1 fusion.10
  177.5 8.2 %all_gather.15 = f32[2,8192]{1,0:T(2,128)S(1)} all-gather(f32[2,2048]{1,0:T(2,128)S(1)} %pad_maximum_fusion), channel_id=1, replica_groups=mesh['tok'=4,'voc'=8] {'tok'}, dimensions={1}, use_global_device_ids=true | all-gather | bytes 81920 | tf_op jit(solution)/shard_map/all_gather | solution.py:156
  185.7 0.1 fusion.17
  185.7 2.0 %gather_fusion.1 = f32[160]{0:T(256)} fusion(f32[8192]{0:T(1024)S(1)} %bitcast.75, s32[1024]{0:T(1024)S(1)} %pad_clamp_fusion), kind=kCustom, calls=%fused_computation.1 | custom fusion | bytes 1920 | tf_op jit(solution)/shard_map/gather | solution.py:161
  187.7 2.0 %gather_fusion = f32[160]{0:T(256)} fusion(f32[8192]{0:T(1024)S(1)} %bitcast.74, s32[1024]{0:T(1024)S(1)} %pad_clamp_fusion), kind=kCustom, calls=%fused_computation | custom fusion | bytes 1920 | tf_op jit(solution)/shard_map/gather | solution.py:161
  (20 shorter events, 0.2 us)
Async XLA Ops:
  7.2 5.8 %copy-start.4 = (s32[8]{0:T(128)S(1)}, s32[8]{0:T(128)}, u32[]{:S(2)}) copy-start(s32[8]{0:T(128)} %param.10) | copy-start | bytes 100
  7.2 6.1 %copy-start.2 = (s32[8]{0:T(128)S(1)}, s32[8]{0:T(128)}, u32[]{:S(2)}) copy-start(s32[8]{0:T(128)} %param.11) | copy-start | bytes 100
  7.2 54.7 %all-gather.3.cloned.1.call-start = ((), (), s32[]{:S(2)}) async-start(), calls=%async_computation | async-start | bytes 4718592 | tf_op jit(solution)/shard_map/all_gather | solution.py:145
  12.2 97.0 %all-gather.5.cloned.1.call-start = ((), (), s32[]{:S(2)}) async-start(), calls=%async_computation.1 | async-start | bytes 4718592 | tf_op jit(solution)/shard_map/all_gather | solution.py:145
  103.9 0.9 copy-start
  151.1 0.8 copy-start.1
  154.6 4.0 %copy-start.3 = (bf16[1024,2048]{1,0:T(8,128)(2,1)S(1)}, bf16[1024,2048]{1,0:T(8,128)(2,1)}, u32[]{:S(2)}) copy-start(bf16[1024,2048]{1,0:T(8,128)(2,1)} %all-gather.5.cloned.1.call-done.x_ref) | copy-start | bytes 12582916
Sparse Core Ops, SparseCore 0:
  12.3 49.5 all-gather.2
  63.5 45.6 all-gather.4

commit v5 on v2

--- a/solution.py
+++ b/solution.py
@@ -23,7 +23,9 @@
 
 def stats_kernel(ncols, x_ref, w_ref, t_ref, m_out, s_out, e_out, p_out, m_sc, s_sc, e_sc, p_sc):
     j = pl.program_id(1)
-    tn = w_ref.shape[1]
+    last = pl.num_programs(1) - 1
+    tn = w_ref.shape[0]
+    lane = m_sc.shape[1]
 
     @pl.when(j == 0)
     def _():
@@ -32,45 +34,72 @@
         e_sc[...] = jnp.zeros(e_sc.shape, jnp.float32)
         p_sc[...] = jnp.zeros(p_sc.shape, jnp.float32)
 
-    logits = jnp.dot(x_ref[...], w_ref[...], preferred_element_type=jnp.float32)
-    cols = j * tn + lax.broadcasted_iota(jnp.int32, logits.shape, 1)
-    logits = jnp.where(cols < ncols, logits, NEG)
-    old = m_sc[...]
-    new = jnp.maximum(old, jnp.max(logits, axis=1, keepdims=True))
-    alpha = jnp.exp(old - new)
-    expo = jnp.exp(logits - new)
-    s_sc[...] = s_sc[...] * alpha + jnp.sum(expo, axis=1, keepdims=True)
-    e_sc[...] = e_sc[...] * alpha + jnp.sum(expo * logits, axis=1, keepdims=True)
-    p_sc[...] = p_sc[...] + jnp.sum(jnp.where(cols == t_ref[...], logits, 0.0), axis=1, keepdims=True)
-    m_sc[...] = new
+    logits = lax.dot_general(
+        x_ref[...], w_ref[...], (((1,), (1,)), ((), ())), preferred_element_type=jnp.float32
+    )
+    lanes = lax.broadcasted_iota(jnp.int32, m_sc.shape, 1)
+    shift = t_ref[...] - j * tn
 
-    @pl.when(j == pl.num_programs(1) - 1)
+    def update(masked):
+        groups = [logits[:, k * lane:(k + 1) * lane] for k in range(tn // lane)]
+        if masked:
+            groups = [jnp.where(lanes < ncols - j * tn - k * lane, g, NEG) for k, g in enumerate(groups)]
+        top = groups[0]
+        for g in groups[1:]:
+            top = jnp.maximum(top, g)
+        old = m_sc[...]
+        new = jnp.maximum(old, top)
+        alpha = jnp.exp(old - new)
+        total = s_sc[...] * alpha
+        moment = e_sc[...] * alpha
+        picked = p_sc[...]
+        for k, g in enumerate(groups):
+            expo = jnp.exp(g - new)
+            total = total + expo
+            moment = moment + expo * g
+            picked = picked + jnp.where(lanes == shift - k * lane, g, 0.0)
+        m_sc[...] = new
+        s_sc[...] = total
+        e_sc[...] = moment
+        p_sc[...] = picked
+
+    if ncols % tn:
+        pl.when(j < last)(lambda: update(False))
+        pl.when(j == last)(lambda: update(True))
+    else:
+        update(False)
+
+    @pl.when(j == last)
     def _():
-        m_out[...] = m_sc[...]
-        s_out[...] = s_sc[...]
-        e_out[...] = e_sc[...]
-        p_out[...] = p_sc[...]
+        m = m_sc[...]
+        top = jnp.max(m, axis=1, keepdims=True)
+        scale = jnp.exp(m - top)
+        m_out[...] = top
+        s_out[...] = jnp.sum(s_sc[...] * scale, axis=1, keepdims=True)
+        e_out[...] = jnp.sum(e_sc[...] * scale, axis=1, keepdims=True)
+        p_out[...] = jnp.sum(p_sc[...], axis=1, keepdims=True)
 
 
-def row_stats(piece, weights, wanted):
+def row_stats(piece, weights_t, wanted):
     rows, depth = piece.shape
-    ncols = weights.shape[1]
+    ncols = weights_t.shape[0]
     tm = min(512, rows)
     tn = TILE_N
-    grid = (rows // tm, pl.cdiv(ncols, tn))
-    wanted = jnp.where((wanted >= 0) & (wanted < ncols), wanted, -1).reshape(rows, 1)
-    row_spec = pl.BlockSpec((tm, 1), lambda i, j: (i, 0))
+    lane = 128
+    steps = pl.cdiv(ncols, tn)
+    wanted = jnp.where((wanted >= 0) & (wanted < ncols), wanted, -1)
+    out_spec = pl.BlockSpec((tm, 1), lambda i, j: (i, 0))
     outs = pl.pallas_call(
         lambda *refs: stats_kernel(ncols, *refs),
-        grid=grid,
+        grid=(rows // tm, steps),
         in_specs=[
             pl.BlockSpec((tm, depth), lambda i, j: (i, 0)),
-            pl.BlockSpec((depth, tn), lambda i, j: (0, j)),
-            row_spec,
+            pl.BlockSpec((tn, depth), lambda i, j: (j, 0)),
+            pl.BlockSpec((tm, lane), lambda i, j: (i, 0)),
         ],
-        out_specs=[row_spec] * 4,
+        out_specs=[out_spec] * 4,
         out_shape=[jax.ShapeDtypeStruct((rows, 1), jnp.float32)] * 4,
-        scratch_shapes=[pltpu.VMEM((tm, 1), jnp.float32)] * 4,
+        scratch_shapes=[pltpu.VMEM((tm, lane), jnp.float32)] * 4,
         compiler_params=pltpu.CompilerParams(
             dimension_semantics=("arbitrary", "arbitrary"), vmem_limit_bytes=48 * 1024 * 1024
         ),
@@ -79,7 +108,7 @@
             transcendentals=rows * ncols,
             bytes_accessed=2 * depth * ncols * (rows // tm) + 2 * rows * depth,
         ),
-    )(piece, weights, wanted)
+    )(piece, weights_t, jnp.broadcast_to(wanted[:, None], (rows, lane)))
     return jnp.stack([o.reshape(rows) for o in outs], axis=0)
 
 
@@ -98,10 +127,11 @@
     step = local // chunks
     wanted = lax.dynamic_slice_in_dim(targets, tok_index * group_rows, group_rows, 0) - col_base
     wanted = wanted.reshape(n_voc, chunks, step)
+    head_t = head.T
     parts = []
     for j in range(chunks):
         piece = lax.all_gather(normed[j * step:(j + 1) * step], "voc", axis=0, tiled=True)
-        parts.append(row_stats(piece, head, wanted[:, j, :].reshape(-1)).reshape(4, n_voc, step))
+        parts.append(row_stats(piece, head_t, wanted[:, j, :].reshape(-1)).reshape(4, n_voc, step))
     stats = jnp.stack(parts, axis=2).reshape(4, group_rows)
     every = lax.all_gather(stats, "voc", axis=0)
     top = jnp.max(every[:, 0], axis=0)

time: 224 us -> 196 us (0.88)
  waiting for transfers between devices: 16.7 us -> 48.5 us
  local copies, waits for them, and re-layouts: 37 us -> 5.73 us
  Pallas kernels: 125 us -> 98.1 us
    all_gather x2, waiting for transfers between devices: 15.9 us -> 47.8 us  [on_device(): lax.all_gather(normed[j * step:(j + 1) * step], 'voc', axis=0, tiled=True)]
    unnamed x5 -> x4, local copies, waits for them, and re-layouts: 31.3 us -> 0.01 us
    pallas_call x2, Pallas kernels: 125 us -> 98.1 us  [row_stats(): pl.pallas_call(lambda *refs: stats_kernel(ncols, *refs), grid=(rows // tm...]
  transfers between devices with their start and end apart: 2 -> 2, of which waited for: 1 -> 1; matrix products, arithmetic and copies ran while one was open for 15% -> 1% of each run, Pallas kernels for 28% -> 25%
where the time goes in v5:
time: 196 us
  Pallas kernels  98.1 us (50%)
  waiting for transfers between devices  48.5 us (25%)
  blocking collectives  22.3 us (11%)
  between operations  14.3 us (7%)
  other arithmetic  6.87 us (4%)
  local copies, waits for them, and re-layouts  5.73 us (3%)
    pallas_call x2, Pallas kernels, row_stats(): pl.pallas_call(lambda *refs: stats_kernel(ncols, *refs), grid=(rows // tm...  98.1 us
    all_gather x2, waiting for transfers between devices, on_device(): lax.all_gather(normed[j * step:(j + 1) * step], 'voc', axis=0, tiled=True)  47.8 us
    all_gather x1, blocking collectives, on_device(): every = lax.all_gather(stats, 'voc', axis=0)  14.2 us
    all_gather x1, blocking collectives, on_device(): both = lax.all_gather(own, 'tok', axis=1, tiled=True)  8.12 us
    gather x2, local copies, waits for them, and re-layouts, on_device(): return (both[0][rows], both[1][rows])  4.05 us
  transfers between devices with their start and end apart: 2, of which 1 were waited for; matrix products, arithmetic and copies ran while one was open for 1% of the time, Pallas kernels for 25%

profile of v5, /device:TPU:0, one launch (start us, length us, event | category | flops | bytes accessed | tf_op | source)
XLA Modules:
  0.0 195.9 jit_solution(18222774760865406504)
XLA Ops:
  7.2 0.0 all-gather.3.cloned.1.call-start
  7.2 0.7 convert_element_type.13
  7.9 1.5 fusion
  9.4 1.5 fusion.2
  11.0 0.0 copy-start.1
  11.0 0.0 copy-start
  11.0 1.2 fusion.9
  12.2 0.0 all-gather.3.cloned.1.call-update
  12.2 0.0 all-gather.5.cloned.1.call-start
  12.2 0.7 all-gather.5.cloned.1.call-update
  13.0 0.0 copy-done.1
  13.0 0.2 reduce-window.9
  13.2 0.1 convert_reduce_fusion
  13.2 0.0 copy-done
  13.3 0.1 select_reduce_fusion.1
  13.4 0.7 dynamic-slice_subtract_fusion
  14.1 47.8 %all-gather.3.cloned.1.call-done.refs_0_ = bf16[1024,2048]{1,0:T(8,128)(2,1)} async-done(((bf16[128,2048]{1,0:T(8,128)(2,1)}), bf16[1024,2048]{1,0:T(8,128)(2,1)}) %all-gather.3.cloned.1.call-update) | async-done | bytes 4194320 | tf_op jit(solution)/shard_map/all_gather | solution.py:133
  61.9 0.2 broadcast_in_dim.28.refs_2_
  62.1 49.1 %shard_map.77 = (f32[1024,1]{1,0:T(8,128)S(1)}, f32[1024,1]{1,0:T(8,128)S(1)}, f32[1024,1]{1,0:T(8,128)S(1)}, f32[1024,1]{1,0:T(8,128)S(1)}) custom-call(bf16[1024,2048]{1,0:T(8,128)(2,1)} %all-gather.3.cloned.1.call-done.refs_0_, bf16[6288,2048]{1,0:T(8,128)(2,1)} %bitcast.60, s32[1024,128]{1,0:T(8,128)S(1)} %broadcast_in_dim.28.refs_2_), custom_call_target="tpu_custom_call" | custom-call | flops 26373783552 | bytes 55705600 | tf_op jit(solution)/shard_map/pallas_call | solution.py:92
  111.2 0.2 reduce.2
  111.5 0.2 reduce.3
  111.7 0.2 reduce.4
  111.9 0.2 reduce.5
  112.1 0.0 all-gather.5.cloned.1.call-done.refs_0_
  112.1 0.2 broadcast_in_dim.29.refs_2_
  112.3 49.0 %shard_map.78 = (f32[1024,1]{1,0:T(8,128)S(1)}, f32[1024,1]{1,0:T(8,128)S(1)}, f32[1024,1]{1,0:T(8,128)S(1)}, f32[1024,1]{1,0:T(8,128)S(1)}) custom-call(bf16[1024,2048]{1,0:T(8,128)(2,1)} %all-gather.5.cloned.1.call-done.refs_0_, bf16[6288,2048]{1,0:T(8,128)(2,1)} %bitcast.61, s32[1024,128]{1,0:T(8,128)S(1)} %broadcast_in_dim.29.refs_2_), custom_call_target="tpu_custom_call" | custom-call | flops 26373783552 | bytes 55705600 | tf_op jit(solution)/shard_map/pallas_call | solution.py:92
  161.3 0.2 reduce.6
  161.5 0.2 reduce.7
  161.7 0.2 reduce.8
  161.9 0.2 reduce.9
  162.2 14.2 %all_gather.14 = f32[8,4,2048]{2,1,0:T(4,128)S(1)} all-gather(f32[1,4,2048]{2,1,0:T(4,128)S(1)} %all_gather_reshape.3), channel_id=1, replica_groups=mesh['tok'=4,'voc'=8] {'voc'}, dimensions={0}, use_global_device_ids=true | all-gather | bytes 294912 | tf_op jit(solution)/shard_map/all_gather | solution.py:136
  176.4 0.2 fusion.10
  176.7 0.1 fusion.4
  176.8 8.1 %all_gather.15 = f32[2,8192]{1,0:T(2,128)S(1)} all-gather(f32[2,2048]{1,0:T(2,128)S(1)} %pad_maximum_fusion), channel_id=1, replica_groups=mesh['tok'=4,'voc'=8] {'tok'}, dimensions={1}, use_global_device_ids=true | all-gather | bytes 81920 | tf_op jit(solution)/shard_map/all_gather | solution.py:144
  184.9 0.1 fusion.11
  185.0 2.0 %gather_fusion.1 = f32[160]{0:T(256)} fusion(f32[8192]{0:T(1024)S(1)} %bitcast.43, s32[1024]{0:T(1024)S(1)} %pad_clamp_fusion), kind=kCustom, calls=%fused_computation.1 | custom fusion | bytes 1920 | tf_op jit(solution)/shard_map/gather | solution.py:149
  187.0 2.0 %gather_fusion = f32[160]{0:T(256)} fusion(f32[8192]{0:T(1024)S(1)} %bitcast.42, s32[1024]{0:T(1024)S(1)} %pad_clamp_fusion), kind=kCustom, calls=%fused_computation | custom fusion | bytes 1920 | tf_op jit(solution)/shard_map/gather | solution.py:149
  (15 shorter events, 0.2 us)
Async XLA Ops:
  7.2 54.8 %all-gather.3.cloned.1.call-start = ((), (), s32[]{:S(2)}) async-start(), calls=%async_computation | async-start | bytes 4718592 | tf_op jit(solution)/shard_map/all_gather | solution.py:133
  11.0 2.0 %copy-start.1 = (s32[8]{0:T(128)S(1)}, s32[8]{0:T(128)}, u32[]{:S(2)}) copy-start(s32[8]{0:T(128)} %param.10) | copy-start | bytes 100
  11.0 2.3 %copy-start = (s32[8]{0:T(128)S(1)}, s32[8]{0:T(128)}, u32[]{:S(2)}) copy-start(s32[8]{0:T(128)} %param.11) | copy-start | bytes 100
  12.2 99.9 %all-gather.5.cloned.1.call-start = ((), (), s32[]{:S(2)}) async-start(), calls=%async_computation.1 | async-start | bytes 4718592 | tf_op jit(solution)/shard_map/all_gather | solution.py:133
Sparse Core Ops, SparseCore 0:
  12.3 49.5 all-gather.2
  63.5 45.6 all-gather.4

commit v6 on v5

--- a/solution.py
+++ b/solution.py
@@ -6,7 +6,7 @@
 from jax.experimental.pallas import tpu as pltpu
 
 MAXLEN = 1024
-CHUNKS = 2
+CHUNKS = 4
 TILE_N = 512
 NEG = -1e30
 
@@ -131,22 +131,23 @@
     parts = []
     for j in range(chunks):
         piece = lax.all_gather(normed[j * step:(j + 1) * step], "voc", axis=0, tiled=True)
-        parts.append(row_stats(piece, head_t, wanted[:, j, :].reshape(-1)).reshape(4, n_voc, step))
-    stats = jnp.stack(parts, axis=2).reshape(4, group_rows)
-    every = lax.all_gather(stats, "voc", axis=0)
-    top = jnp.max(every[:, 0], axis=0)
-    factor = jnp.exp(every[:, 0] - top[None, :])
-    total = jnp.sum(every[:, 1] * factor, axis=0)
-    moment = jnp.sum(every[:, 2] * factor, axis=0)
-    picked = jnp.sum(every[:, 3], axis=0)
-    lse = top + jnp.log(total)
-    own = jnp.stack([picked - lse, lse - moment / total], axis=0)
+        stats = row_stats(piece, head_t, wanted[:, j, :].reshape(-1))
+        every = lax.all_gather(stats, "voc", axis=0)
+        top = jnp.max(every[:, 0], axis=0)
+        factor = jnp.exp(every[:, 0] - top[None, :])
+        total = jnp.sum(every[:, 1] * factor, axis=0)
+        moment = jnp.sum(every[:, 2] * factor, axis=0)
+        picked = jnp.sum(every[:, 3], axis=0)
+        lse = top + jnp.log(total)
+        parts.append(jnp.stack([picked - lse, lse - moment / total], axis=0).reshape(2, n_voc, step))
+    own = jnp.stack(parts, axis=2).reshape(2, group_rows)
     both = lax.all_gather(own, "tok", axis=1, tiled=True)
     out_rows = targets.shape[0] * 5 // 8 // (n_tok * n_voc)
     device = lax.axis_index(("tok", "voc"))
     positions = device * out_rows + jnp.arange(out_rows, dtype=jnp.int32)
     rows = slot_rows(positions, lengths, perm)
-    return (both[0][rows], both[1][rows])
+    picked_out = jnp.take(both, rows, axis=1)
+    return (picked_out[0], picked_out[1])
 
 
 def solution(mesh):

time: 196 us -> 265 us (1.35)
  blocking collectives: 22.3 us -> 98 us
  waiting for transfers between devices: 48.5 us -> 33.5 us
  local copies, waits for them, and re-layouts: 5.73 us -> 13.1 us
    all_gather x1 -> x4, blocking collectives: 14.2 us -> 56.6 us  [on_device(): every = lax.all_gather(stats, 'voc', axis=0)]
    all_gather x1, blocking collectives: 8.12 us -> 41.4 us  [on_device(): both = lax.all_gather(own, 'tok', axis=1, tiled=True)]
    all_gather x2 -> x4, waiting for transfers between devices: 47.8 us -> 31.6 us  [on_device(): lax.all_gather(normed[j * step:(j + 1) * step], 'voc', axis=0, tiled=True)]
    unnamed x4 -> x12, local copies, waits for them, and re-layouts: 0.01 us -> 6.39 us
    pallas_call x2 -> x4, Pallas kernels: 98.1 us -> 98.4 us  [row_stats(): pl.pallas_call(lambda *refs: stats_kernel(ncols, *refs), grid=(rows // tm...]
  transfers between devices with their start and end apart: 2 -> 4, of which waited for: 1 -> 2; matrix products, arithmetic and copies ran while one was open for 1% -> 2% of each run, Pallas kernels for 25% -> 28%
where the time goes in v6:
time: 265 us
  Pallas kernels  98.4 us (37%)
  blocking collectives  98 us (37%)
  waiting for transfers between devices  33.5 us (13%)
  between operations  14 us (5%)
  local copies, waits for them, and re-layouts  13.1 us (5%)
  other arithmetic  7.8 us (3%)
    pallas_call x4, Pallas kernels, row_stats(): pl.pallas_call(lambda *refs: stats_kernel(ncols, *refs), grid=(rows // tm...  98.4 us
    all_gather x4, blocking collectives, on_device(): every = lax.all_gather(stats, 'voc', axis=0)  56.6 us
    all_gather x1, blocking collectives, on_device(): both = lax.all_gather(own, 'tok', axis=1, tiled=True)  41.4 us
    all_gather x4, waiting for transfers between devices, on_device(): lax.all_gather(normed[j * step:(j + 1) * step], 'voc', axis=0, tiled=True)  31.6 us
    unnamed x12, local copies, waits for them, and re-layouts  6.39 us
  transfers between devices with their start and end apart: 4, of which 2 were waited for; matrix products, arithmetic and copies ran while one was open for 2% of the time, Pallas kernels for 28%

profile of v6, /device:TPU:0, one launch (start us, length us, event | category | flops | bytes accessed | tf_op | source)
XLA Modules:
  0.0 264.9 jit_solution(2872381350454617555)
XLA Ops:
  7.2 0.7 convert_element_type.14
  7.9 1.5 fusion
  9.4 1.5 fusion.2
  11.0 1.1 fusion.27
  12.2 0.7 all-gather.13.cloned.1.call-update
  12.9 0.7 all-gather.19.cloned.1.call-update
  13.6 0.5 all-gather.17.cloned.1.call-update
  14.2 0.7 dynamic-slice_subtract_fusion
  15.4 0.2 reduce-window.9
  15.8 28.3 %all-gather.15.cloned.1.call-done.refs_0_ = bf16[512,2048]{1,0:T(8,128)(2,1)} async-done(((bf16[64,2048]{1,0:T(8,128)(2,1)}), bf16[512,2048]{1,0:T(8,128)(2,1)}) %all-gather.15.cloned.1.call-update) | async-done | bytes 2097168 | tf_op jit(solution)/shard_map/all_gather | solution.py:133
  44.1 0.1 broadcast_in_dim.79.refs_2_
  44.3 1.6 copy-done.3
  45.9 24.6 %shard_map.78 = (f32[512,1]{1,0:T(8,128)S(1)}, f32[512,1]{1,0:T(8,128)S(1)}, f32[512,1]{1,0:T(8,128)S(1)}, f32[512,1]{1,0:T(8,128)S(1)}) custom-call(bf16[512,2048]{1,0:T(8,128)(2,1)S(1)} %copy-done.3, bf16[6288,2048]{1,0:T(8,128)(2,1)} %bitcast.134, s32[512,128]{1,0:T(8,128)S(1)} %broadcast_in_dim.79.refs_2_), custom_call_target="tpu_custom_call" | custom-call | flops 13186891776 | bytes 27852800 | tf_op jit(solution)/shard_map/pallas_call | solution.py:92
  70.5 0.1 reduce.14
  70.6 0.1 reduce.15
  70.8 0.1 reduce.16
  70.9 0.1 reduce.17
  71.1 3.3 %all-gather.13.cloned.1.call-done.refs_0_ = bf16[512,2048]{1,0:T(8,128)(2,1)} async-done(((bf16[64,2048]{1,0:T(8,128)(2,1)}), bf16[512,2048]{1,0:T(8,128)(2,1)}) %all-gather.13.cloned.1.call-update) | async-done | bytes 2097168 | tf_op jit(solution)/shard_map/all_gather | solution.py:133
  74.5 1.6 copy-done.2
  76.0 24.6 %shard_map.77 = (f32[512,1]{1,0:T(8,128)S(1)}, f32[512,1]{1,0:T(8,128)S(1)}, f32[512,1]{1,0:T(8,128)S(1)}, f32[512,1]{1,0:T(8,128)S(1)}) custom-call(bf16[512,2048]{1,0:T(8,128)(2,1)S(1)} %copy-done.2, bf16[6288,2048]{1,0:T(8,128)(2,1)} %bitcast.135, s32[512,128]{1,0:T(8,128)S(1)} %broadcast_in_dim.78.refs_2_), custom_call_target="tpu_custom_call" | custom-call | flops 13186891776 | bytes 27852800 | tf_op jit(solution)/shard_map/pallas_call | solution.py:92
  100.7 0.1 reduce.9
  100.8 0.1 reduce.10
  100.9 0.1 reduce.11
  101.1 0.1 reduce.12
  101.3 14.0 %all-gather.5 = f32[8,4,512]{2,1,0:T(4,128)S(1)} all-gather(f32[1,4,512]{2,1,0:T(4,128)S(1)} %maximum_bitcast_fusion.1), channel_id=3, replica_groups=mesh['tok'=4,'voc'=8] {'voc'}, dimensions={0}, use_global_device_ids=true | all-gather | bytes 73728 | tf_op jit(solution)/shard_map/all_gather | solution.py:135
  115.3 14.5 %all-gather.4 = f32[8,4,512]{2,1,0:T(4,128)S(1)} all-gather(f32[1,4,512]{2,1,0:T(4,128)S(1)} %maximum_bitcast_fusion), channel_id=2, replica_groups=mesh['tok'=4,'voc'=8] {'voc'}, dimensions={0}, use_global_device_ids=true | all-gather | bytes 73728 | tf_op jit(solution)/shard_map/all_gather | solution.py:135
  129.7 0.1 fusion.28
  130.3 0.1 broadcast_in_dim.81.refs_2_
  130.4 1.6 copy-done.1
  132.0 24.6 %shard_map.80 = (f32[512,1]{1,0:T(8,128)S(1)}, f32[512,1]{1,0:T(8,128)S(1)}, f32[512,1]{1,0:T(8,128)S(1)}, f32[512,1]{1,0:T(8,128)S(1)}) custom-call(bf16[512,2048]{1,0:T(8,128)(2,1)S(1)} %copy-done.1, bf16[6288,2048]{1,0:T(8,128)(2,1)} %bitcast.136, s32[512,128]{1,0:T(8,128)S(1)} %broadcast_in_dim.81.refs_2_), custom_call_target="tpu_custom_call" | custom-call | flops 13186891776 | bytes 27852800 | tf_op jit(solution)/shard_map/pallas_call | solution.py:92
  156.6 0.1 reduce.24
  156.8 0.1 reduce.25
  156.9 0.1 reduce.26
  157.1 0.1 reduce.27
  157.2 14.2 %all-gather.7 = f32[8,4,512]{2,1,0:T(4,128)S(1)} all-gather(f32[1,4,512]{2,1,0:T(4,128)S(1)} %maximum_bitcast_fusion.3), channel_id=5, replica_groups=mesh['tok'=4,'voc'=8] {'voc'}, dimensions={0}, use_global_device_ids=true | all-gather | bytes 73728 | tf_op jit(solution)/shard_map/all_gather | solution.py:135
  171.4 0.1 broadcast_in_dim.80.refs_2_
  171.6 1.6 copy-done
  173.1 24.6 %shard_map.79 = (f32[512,1]{1,0:T(8,128)S(1)}, f32[512,1]{1,0:T(8,128)S(1)}, f32[512,1]{1,0:T(8,128)S(1)}, f32[512,1]{1,0:T(8,128)S(1)}) custom-call(bf16[512,2048]{1,0:T(8,128)(2,1)S(1)} %copy-done, bf16[6288,2048]{1,0:T(8,128)(2,1)} %bitcast.137, s32[512,128]{1,0:T(8,128)S(1)} %broadcast_in_dim.80.refs_2_), custom_call_target="tpu_custom_call" | custom-call | flops 13186891776 | bytes 27852800 | tf_op jit(solution)/shard_map/pallas_call | solution.py:92
  197.8 0.1 reduce.19
  197.9 0.1 reduce.20
  198.0 0.1 reduce.21
  198.2 0.1 reduce.22
  198.4 14.0 %all-gather.6 = f32[8,4,512]{2,1,0:T(4,128)S(1)} all-gather(f32[1,4,512]{2,1,0:T(4,128)S(1)} %maximum_bitcast_fusion.2), channel_id=4, replica_groups=mesh['tok'=4,'voc'=8] {'voc'}, dimensions={0}, use_global_device_ids=true | all-gather | bytes 73728 | tf_op jit(solution)/shard_map/all_gather | solution.py:135
  212.4 0.1 fusion.30
  212.9 0.4 copy.42
  213.3 41.4 %all_gather.51 = f32[2,8192]{0,1:T(8,128)} all-gather(f32[2,2048]{0,1:T(8,128)S(1)} %bitcast.114), channel_id=1, replica_groups=mesh['tok'=4,'voc'=8] {'tok'}, dimensions={1}, use_global_device_ids=true | all-gather | bytes 81920 | tf_op jit(solution)/shard_map/all_gather | solution.py:144
  254.7 2.9 %gather_fusion = f32[160,2]{1,0:T(8,128)S(1)} fusion(f32[2,8192]{0,1:T(8,128)} %all_gather.51, s32[1024]{0:T(1024)S(1)} %pad_clamp_fusion), kind=kCustom, calls=%fused_computation | custom fusion | bytes 3200 | tf_op jit(solution)/shard_map/jit(_take)/gather | solution.py:149
  257.6 0.8 slice_reduce_fusion
  (58 shorter events, 1.9 us)
Async XLA Ops:
  7.2 37.0 %all-gather.15.cloned.1.call-start = ((), (), s32[]{:S(2)}) async-start(), calls=%async_computation.1 | async-start | bytes 2359296 | tf_op jit(solution)/shard_map/all_gather | solution.py:133
  11.0 4.4 %copy-start.5 = (s32[8]{0:T(128)S(1)}, s32[8]{0:T(128)}, u32[]{:S(2)}) copy-start(s32[8]{0:T(128)} %param.10) | copy-start | bytes 100
  11.0 4.7 %copy-start.4 = (s32[8]{0:T(128)S(1)}, s32[8]{0:T(128)}, u32[]{:S(2)}) copy-start(s32[8]{0:T(128)} %param.11) | copy-start | bytes 100
  12.1 62.2 %all-gather.13.cloned.1.call-start = ((), (), s32[]{:S(2)}) async-start(), calls=%async_computation | async-start | bytes 2359296 | tf_op jit(solution)/shard_map/all_gather | solution.py:133
  12.9 117.4 %all-gather.19.cloned.1.call-start = ((), (), s32[]{:S(2)}) async-start(), calls=%async_computation.3 | async-start | bytes 2359296 | tf_op jit(solution)/shard_map/all_gather | solution.py:133
  13.6 157.8 %all-gather.17.cloned.1.call-start = ((), (), s32[]{:S(2)}) async-start(), calls=%async_computation.2 | async-start | bytes 2359296 | tf_op jit(solution)/shard_map/all_gather | solution.py:133
  44.3 1.6 copy-start.3
  74.4 1.6 copy-start.2
  130.4 1.6 copy-start.1
  171.5 1.6 copy-start
Sparse Core Ops, SparseCore 0:
  12.2 31.8 all-gather.14
  45.7 28.5 all-gather.12
  75.9 28.5 all-gather.18
  106.0 29.0 all-gather.16

commit v7 on v5

--- a/solution.py
+++ b/solution.py
@@ -113,12 +113,14 @@
 
 
 def on_device(hidden, gain, head, targets, lengths, perm):
-    values = hidden.astype(jnp.float32)
-    scale = lax.rsqrt(jnp.mean(values * values, axis=1, keepdims=True) + 1e-06)
-    normed = (values * scale * gain.astype(jnp.float32)[None, :]).astype(jnp.bfloat16)
+    def norm(part):
+        values = part.astype(jnp.float32)
+        scale = lax.rsqrt(jnp.mean(values * values, axis=1, keepdims=True) + 1e-06)
+        return (values * scale * gain.astype(jnp.float32)[None, :]).astype(jnp.bfloat16)
+
     n_tok = lax.axis_size("tok")
     n_voc = lax.axis_size("voc")
-    local = normed.shape[0]
+    local = hidden.shape[0]
     group_rows = local * n_voc
     shard_cols = head.shape[1]
     col_base = lax.axis_index("voc") * shard_cols
@@ -130,7 +132,7 @@
     head_t = head.T
     parts = []
     for j in range(chunks):
-        piece = lax.all_gather(normed[j * step:(j + 1) * step], "voc", axis=0, tiled=True)
+        piece = lax.all_gather(norm(hidden[j * step:(j + 1) * step]), "voc", axis=0, tiled=True)
         parts.append(row_stats(piece, head_t, wanted[:, j, :].reshape(-1)).reshape(4, n_voc, step))
     stats = jnp.stack(parts, axis=2).reshape(4, group_rows)
     every = lax.all_gather(stats, "voc", axis=0)
@@ -146,7 +148,8 @@
     device = lax.axis_index(("tok", "voc"))
     positions = device * out_rows + jnp.arange(out_rows, dtype=jnp.int32)
     rows = slot_rows(positions, lengths, perm)
-    return (both[0][rows], both[1][rows])
+    picked_out = jnp.take(both, rows, axis=1)
+    return (picked_out[0], picked_out[1])
 
 
 def solution(mesh):

time: 196 us -> 229 us (1.17)
  blocking collectives: 22.3 us -> 55.5 us
    all_gather x1, blocking collectives: 8.12 us -> 41.3 us  [on_device(): both = lax.all_gather(own, 'tok', axis=1, tiled=True)]
  transfers between devices with their start and end apart: 2 -> 2, of which waited for: 1 -> 1; matrix products, arithmetic and copies ran while one was open for 1% -> 1% of each run, Pallas kernels for 25% -> 21%
where the time goes in v7:
time: 229 us
  Pallas kernels  98.1 us (43%)
  blocking collectives  55.5 us (24%)
  waiting for transfers between devices  48.5 us (21%)
  between operations  14.3 us (6%)
  other arithmetic  7.98 us (3%)
  local copies, waits for them, and re-layouts  4.46 us (2%)
    pallas_call x2, Pallas kernels, row_stats(): pl.pallas_call(lambda *refs: stats_kernel(ncols, *refs), grid=(rows // tm...  98.1 us
    all_gather x2, waiting for transfers between devices, on_device(): lax.all_gather(norm(hidden[j * step:(j + 1) * step]), 'voc', axis=0, tile...  47.8 us
    all_gather x1, blocking collectives, on_device(): both = lax.all_gather(own, 'tok', axis=1, tiled=True)  41.3 us
    all_gather x1, blocking collectives, on_device(): every = lax.all_gather(stats, 'voc', axis=0)  14.2 us
  transfers between devices with their start and end apart: 2, of which 1 were waited for; matrix products, arithmetic and copies ran while one was open for 1% of the time, Pallas kernels for 21%

profile of v7, /device:TPU:0, one launch (start us, length us, event | category | flops | bytes accessed | tf_op | source)
XLA Modules:
  0.0 228.9 jit_solution(12397844941872413437)
XLA Ops:
  7.2 0.0 copy-start.1
  7.2 0.0 copy-start
  7.2 0.0 all-gather.3.cloned.1.call-start
  7.2 1.5 fusion
  8.7 0.7 convert_element_type.21
  9.4 2.6 %fusion.2 = (bf16[128,2048]{1,0:T(8,128)(2,1)}, bf16[128,2048]{1,0:T(8,128)(2,1)}) fusion(f32[2048]{0:T(1024)S(1)} %convert_element_type.21, f32[128]{0:T(128)S(1)} %get-tuple-element.40, bf16[256,2048]{1,0:T(8,128)(2,1)} %param.6, f32[128]{0:T(128)S(1)} %get-tuple-element.39), kind=kLoop, calls=%fused_computation.7 | loop fusion | flops 2097152 | bytes 2106368 | tf_op jit(solution)/shard_map/convert_element_type | solution.py:119
  12.0 0.0 all-gather.3.cloned.1.call-update
  12.0 0.0 all-gather.5.cloned.1.call-start
  12.1 0.7 all-gather.5.cloned.1.call-update
  12.8 0.0 copy-done.1
  12.8 0.2 reduce-window.9
  13.0 0.1 convert_reduce_fusion
  13.1 0.0 copy-done
  13.1 0.1 select_reduce_fusion.1
  13.2 0.7 dynamic-slice_subtract_fusion
  14.0 47.8 %all-gather.3.cloned.1.call-done.refs_0_ = bf16[1024,2048]{1,0:T(8,128)(2,1)} async-done(((bf16[128,2048]{1,0:T(8,128)(2,1)}), bf16[1024,2048]{1,0:T(8,128)(2,1)}) %all-gather.3.cloned.1.call-update) | async-done | bytes 4194320 | tf_op jit(solution)/shard_map/all_gather | solution.py:135
  61.8 0.2 broadcast_in_dim.63.refs_2_
  62.0 49.1 %shard_map.77 = (f32[1024,1]{1,0:T(8,128)S(1)}, f32[1024,1]{1,0:T(8,128)S(1)}, f32[1024,1]{1,0:T(8,128)S(1)}, f32[1024,1]{1,0:T(8,128)S(1)}) custom-call(bf16[1024,2048]{1,0:T(8,128)(2,1)} %all-gather.3.cloned.1.call-done.refs_0_, bf16[6288,2048]{1,0:T(8,128)(2,1)} %bitcast.58, s32[1024,128]{1,0:T(8,128)S(1)} %broadcast_in_dim.63.refs_2_), custom_call_target="tpu_custom_call" | custom-call | flops 26373783552 | bytes 55705600 | tf_op jit(solution)/shard_map/pallas_call | solution.py:92
  111.1 0.2 reduce.2
  111.3 0.2 reduce.3
  111.5 0.2 reduce.4
  111.7 0.2 reduce.5
  111.9 0.0 all-gather.5.cloned.1.call-done.refs_0_
  112.0 0.2 broadcast_in_dim.64.refs_2_
  112.1 49.0 %shard_map.78 = (f32[1024,1]{1,0:T(8,128)S(1)}, f32[1024,1]{1,0:T(8,128)S(1)}, f32[1024,1]{1,0:T(8,128)S(1)}, f32[1024,1]{1,0:T(8,128)S(1)}) custom-call(bf16[1024,2048]{1,0:T(8,128)(2,1)} %all-gather.5.cloned.1.call-done.refs_0_, bf16[6288,2048]{1,0:T(8,128)(2,1)} %bitcast.59, s32[1024,128]{1,0:T(8,128)S(1)} %broadcast_in_dim.64.refs_2_), custom_call_target="tpu_custom_call" | custom-call | flops 26373783552 | bytes 55705600 | tf_op jit(solution)/shard_map/pallas_call | solution.py:92
  161.1 0.2 reduce.6
  161.3 0.2 reduce.7
  161.5 0.2 reduce.8
  161.8 0.2 reduce.9
  162.1 14.2 %all_gather.14 = f32[8,4,2048]{2,1,0:T(4,128)S(1)} all-gather(f32[1,4,2048]{2,1,0:T(4,128)S(1)} %all_gather_reshape.3), channel_id=1, replica_groups=mesh['tok'=4,'voc'=8] {'voc'}, dimensions={0}, use_global_device_ids=true | all-gather | bytes 294912 | tf_op jit(solution)/shard_map/all_gather | solution.py:138
  176.2 0.2 fusion.12
  176.5 0.1 fusion.7
  176.6 0.4 copy.22
  177.0 41.3 %all_gather.15 = f32[2,8192]{0,1:T(8,128)} all-gather(f32[2,2048]{0,1:T(8,128)S(1)} %copy.22), channel_id=1, replica_groups=mesh['tok'=4,'voc'=8] {'tok'}, dimensions={1}, use_global_device_ids=true | all-gather | bytes 81920 | tf_op jit(solution)/shard_map/all_gather | solution.py:146
  218.3 2.9 %gather_fusion = f32[160,2]{1,0:T(8,128)S(1)} fusion(f32[2,8192]{0,1:T(8,128)} %all_gather.15, s32[1024]{0:T(1024)S(1)} %pad_clamp_fusion), kind=kCustom, calls=%fused_computation | custom fusion | bytes 3200 | tf_op jit(solution)/shard_map/jit(_take)/gather | solution.py:151
  221.1 0.1 select_bitcast_fusion
  221.2 0.8 slice_reduce_fusion
  (16 shorter events, 0.2 us)
Async XLA Ops:
  7.2 5.6 %copy-start.1 = (s32[8]{0:T(128)S(1)}, s32[8]{0:T(128)}, u32[]{:S(2)}) copy-start(s32[8]{0:T(128)} %param.10) | copy-start | bytes 100
  7.2 5.9 %copy-start = (s32[8]{0:T(128)S(1)}, s32[8]{0:T(128)}, u32[]{:S(2)}) copy-start(s32[8]{0:T(128)} %param.11) | copy-start | bytes 100
  7.2 54.6 %all-gather.3.cloned.1.call-start = ((), (), s32[]{:S(2)}) async-start(), calls=%async_computation | async-start | bytes 4718592 | tf_op jit(solution)/shard_map/all_gather | solution.py:135
  12.0 99.9 %all-gather.5.cloned.1.call-start = ((), (), s32[]{:S(2)}) async-start(), calls=%async_computation.1 | async-start | bytes 4718592 | tf_op jit(solution)/shard_map/all_gather | solution.py:135
Sparse Core Ops, SparseCore 0:
  12.1 49.5 all-gather.2
  63.4 45.6 all-gather.4

commit v8 on v5

--- a/solution.py
+++ b/solution.py
@@ -34,31 +34,42 @@
         e_sc[...] = jnp.zeros(e_sc.shape, jnp.float32)
         p_sc[...] = jnp.zeros(p_sc.shape, jnp.float32)
 
-    logits = lax.dot_general(
-        x_ref[...], w_ref[...], (((1,), (1,)), ((), ())), preferred_element_type=jnp.float32
-    )
+    halves = 2
+    width = tn // halves
+    x = x_ref[...]
     lanes = lax.broadcasted_iota(jnp.int32, m_sc.shape, 1)
     shift = t_ref[...] - j * tn
 
     def update(masked):
-        groups = [logits[:, k * lane:(k + 1) * lane] for k in range(tn // lane)]
-        if masked:
-            groups = [jnp.where(lanes < ncols - j * tn - k * lane, g, NEG) for k, g in enumerate(groups)]
-        top = groups[0]
-        for g in groups[1:]:
-            top = jnp.maximum(top, g)
+        total = s_sc[...]
+        moment = e_sc[...]
+        picked = p_sc[...]
         old = m_sc[...]
-        new = jnp.maximum(old, top)
-        alpha = jnp.exp(old - new)
-        total = s_sc[...] * alpha
-        moment = e_sc[...] * alpha
-        picked = p_sc[...]
-        for k, g in enumerate(groups):
-            expo = jnp.exp(g - new)
-            total = total + expo
-            moment = moment + expo * g
-            picked = picked + jnp.where(lanes == shift - k * lane, g, 0.0)
-        m_sc[...] = new
+        for h in range(halves):
+            part = lax.dot_general(
+                x, w_ref[h * width:(h + 1) * width, :], (((1,), (1,)), ((), ())),
+                preferred_element_type=jnp.float32,
+            )
+            base = h * width
+            groups = [part[:, k * lane:(k + 1) * lane] for k in range(width // lane)]
+            if masked:
+                groups = [
+                    jnp.where(lanes < ncols - j * tn - base - k * lane, g, NEG) for k, g in enumerate(groups)
+                ]
+            top = groups[0]
+            for g in groups[1:]:
+                top = jnp.maximum(top, g)
+            new = jnp.maximum(old, top)
+            alpha = jnp.exp(old - new)
+            total = total * alpha
+            moment = moment * alpha
+            for k, g in enumerate(groups):
+                expo = jnp.exp(g - new)
+                total = total + expo
+                moment = moment + expo * g
+                picked = picked + jnp.where(lanes == shift - base - k * lane, g, 0.0)
+            old = new
+        m_sc[...] = old
         s_sc[...] = total
         e_sc[...] = moment
         p_sc[...] = picked

time: 196 us -> 198 us (1.010)
  no operation moved by 1% of the time
where the time goes in v8:
time: 198 us
  Pallas kernels  99.8 us (50%)
  waiting for transfers between devices  48.5 us (24%)
  blocking collectives  22.3 us (11%)
  between operations  14.3 us (7%)
  other arithmetic  6.87 us (3%)
  local copies, waits for them, and re-layouts  5.73 us (3%)
    pallas_call x2, Pallas kernels, row_stats(): pl.pallas_call(lambda *refs: stats_kernel(ncols, *refs), grid=(rows // tm...  99.8 us
    all_gather x2, waiting for transfers between devices, on_device(): lax.all_gather(normed[j * step:(j + 1) * step], 'voc', axis=0, tiled=True)  47.8 us
    all_gather x1, blocking collectives, on_device(): every = lax.all_gather(stats, 'voc', axis=0)  14.2 us
    all_gather x1, blocking collectives, on_device(): both = lax.all_gather(own, 'tok', axis=1, tiled=True)  8.11 us
    gather x2, local copies, waits for them, and re-layouts, on_device(): return (both[0][rows], both[1][rows])  4.05 us
  transfers between devices with their start and end apart: 2, of which 1 were waited for; matrix products, arithmetic and copies ran while one was open for 1% of the time, Pallas kernels for 25%

profile of v8, /device:TPU:0, one launch (start us, length us, event | category | flops | bytes accessed | tf_op | source)
XLA Modules:
  0.0 197.6 jit_solution(11134002463580917365)
XLA Ops:
  7.2 0.0 all-gather.3.cloned.1.call-start
  7.2 0.7 convert_element_type.13
  7.9 1.5 fusion
  9.4 1.5 fusion.2
  11.0 0.0 copy-start.1
  11.0 0.0 copy-start
  11.0 1.2 fusion.9
  12.2 0.0 all-gather.3.cloned.1.call-update
  12.2 0.0 all-gather.5.cloned.1.call-start
  12.2 0.7 all-gather.5.cloned.1.call-update
  13.0 0.0 copy-done.1
  13.0 0.2 reduce-window.9
  13.2 0.1 convert_reduce_fusion
  13.2 0.0 copy-done
  13.3 0.1 select_reduce_fusion.1
  13.4 0.7 dynamic-slice_subtract_fusion
  14.1 47.8 %all-gather.3.cloned.1.call-done.refs_0_ = bf16[1024,2048]{1,0:T(8,128)(2,1)} async-done(((bf16[128,2048]{1,0:T(8,128)(2,1)}), bf16[1024,2048]{1,0:T(8,128)(2,1)}) %all-gather.3.cloned.1.call-update) | async-done | bytes 4194320 | tf_op jit(solution)/shard_map/all_gather | solution.py:144
  61.9 0.2 broadcast_in_dim.28.refs_2_
  62.1 50.0 %shard_map.77 = (f32[1024,1]{1,0:T(8,128)S(1)}, f32[1024,1]{1,0:T(8,128)S(1)}, f32[1024,1]{1,0:T(8,128)S(1)}, f32[1024,1]{1,0:T(8,128)S(1)}) custom-call(bf16[1024,2048]{1,0:T(8,128)(2,1)} %all-gather.3.cloned.1.call-done.refs_0_, bf16[6288,2048]{1,0:T(8,128)(2,1)} %bitcast.60, s32[1024,128]{1,0:T(8,128)S(1)} %broadcast_in_dim.28.refs_2_), custom_call_target="tpu_custom_call" | custom-call | flops 26373783552 | bytes 55705600 | tf_op jit(solution)/shard_map/pallas_call | solution.py:103
  112.1 0.2 reduce.2
  112.3 0.2 reduce.3
  112.5 0.2 reduce.4
  112.8 0.2 reduce.5
  113.0 0.0 all-gather.5.cloned.1.call-done.refs_0_
  113.0 0.2 broadcast_in_dim.29.refs_2_
  113.2 49.8 %shard_map.78 = (f32[1024,1]{1,0:T(8,128)S(1)}, f32[1024,1]{1,0:T(8,128)S(1)}, f32[1024,1]{1,0:T(8,128)S(1)}, f32[1024,1]{1,0:T(8,128)S(1)}) custom-call(bf16[1024,2048]{1,0:T(8,128)(2,1)} %all-gather.5.cloned.1.call-done.refs_0_, bf16[6288,2048]{1,0:T(8,128)(2,1)} %bitcast.61, s32[1024,128]{1,0:T(8,128)S(1)} %broadcast_in_dim.29.refs_2_), custom_call_target="tpu_custom_call" | custom-call | flops 26373783552 | bytes 55705600 | tf_op jit(solution)/shard_map/pallas_call | solution.py:103
  163.0 0.2 reduce.6
  163.2 0.2 reduce.7
  163.5 0.2 reduce.8
  163.7 0.2 reduce.9
  164.0 14.2 %all_gather.14 = f32[8,4,2048]{2,1,0:T(4,128)S(1)} all-gather(f32[1,4,2048]{2,1,0:T(4,128)S(1)} %all_gather_reshape.3), channel_id=1, replica_groups=mesh['tok'=4,'voc'=8] {'voc'}, dimensions={0}, use_global_device_ids=true | all-gather | bytes 294912 | tf_op jit(solution)/shard_map/all_gather | solution.py:147
  178.2 0.2 fusion.10
  178.4 0.1 fusion.4
  178.5 8.1 %all_gather.15 = f32[2,8192]{1,0:T(2,128)S(1)} all-gather(f32[2,2048]{1,0:T(2,128)S(1)} %pad_maximum_fusion), channel_id=1, replica_groups=mesh['tok'=4,'voc'=8] {'tok'}, dimensions={1}, use_global_device_ids=true | all-gather | bytes 81920 | tf_op jit(solution)/shard_map/all_gather | solution.py:155
  186.7 0.1 fusion.11
  186.7 2.0 %gather_fusion.1 = f32[160]{0:T(256)} fusion(f32[8192]{0:T(1024)S(1)} %bitcast.43, s32[1024]{0:T(1024)S(1)} %pad_clamp_fusion), kind=kCustom, calls=%fused_computation.1 | custom fusion | bytes 1920 | tf_op jit(solution)/shard_map/gather | solution.py:160
  188.7 2.0 %gather_fusion = f32[160]{0:T(256)} fusion(f32[8192]{0:T(1024)S(1)} %bitcast.42, s32[1024]{0:T(1024)S(1)} %pad_clamp_fusion), kind=kCustom, calls=%fused_computation | custom fusion | bytes 1920 | tf_op jit(solution)/shard_map/gather | solution.py:160
  (15 shorter events, 0.2 us)
Async XLA Ops:
  7.2 54.8 %all-gather.3.cloned.1.call-start = ((), (), s32[]{:S(2)}) async-start(), calls=%async_computation | async-start | bytes 4718592 | tf_op jit(solution)/shard_map/all_gather | solution.py:144
  11.0 2.0 %copy-start.1 = (s32[8]{0:T(128)S(1)}, s32[8]{0:T(128)}, u32[]{:S(2)}) copy-start(s32[8]{0:T(128)} %param.10) | copy-start | bytes 100
  11.0 2.3 %copy-start = (s32[8]{0:T(128)S(1)}, s32[8]{0:T(128)}, u32[]{:S(2)}) copy-start(s32[8]{0:T(128)} %param.11) | copy-start | bytes 100
  12.2 100.8 %all-gather.5.cloned.1.call-start = ((), (), s32[]{:S(2)}) async-start(), calls=%async_computation.1 | async-start | bytes 4718592 | tf_op jit(solution)/shard_map/all_gather | solution.py:144
Sparse Core Ops, SparseCore 0:
  12.3 49.5 all-gather.2
  63.5 45.6 all-gather.4

commit v9 on v7

--- a/solution.py
+++ b/solution.py
@@ -6,7 +6,6 @@
 from jax.experimental.pallas import tpu as pltpu
 
 MAXLEN = 1024
-CHUNKS = 2
 TILE_N = 512
 NEG = -1e30
 
@@ -83,7 +82,7 @@
 def row_stats(piece, weights_t, wanted):
     rows, depth = piece.shape
     ncols = weights_t.shape[0]
-    tm = min(512, rows)
+    tm = rows if rows <= 512 else (rows // 2 if rows % 16 == 0 and rows <= 1024 else 512)
     tn = TILE_N
     lane = 128
     steps = pl.cdiv(ncols, tn)
@@ -125,16 +124,20 @@
     shard_cols = head.shape[1]
     col_base = lax.axis_index("voc") * shard_cols
     tok_index = lax.axis_index("tok")
-    chunks = CHUNKS if local % (CHUNKS * 8) == 0 else 1
-    step = local // chunks
+    unit = local // 8
+    bounds = [0, 2 * unit, 5 * unit, local] if local % 64 == 0 else [0, local]
     wanted = lax.dynamic_slice_in_dim(targets, tok_index * group_rows, group_rows, 0) - col_base
-    wanted = wanted.reshape(n_voc, chunks, step)
+    wanted = wanted.reshape(n_voc, local)
     head_t = head.T
     parts = []
-    for j in range(chunks):
-        piece = lax.all_gather(norm(hidden[j * step:(j + 1) * step]), "voc", axis=0, tiled=True)
-        parts.append(row_stats(piece, head_t, wanted[:, j, :].reshape(-1)).reshape(4, n_voc, step))
-    stats = jnp.stack(parts, axis=2).reshape(4, group_rows)
+    rest = hidden
+    for lo, hi in zip(bounds[:-1], bounds[1:]):
+        normed = norm(rest[lo:hi])
+        normed, rest = lax.optimization_barrier((normed, rest))
+        piece = lax.all_gather(normed, "voc", axis=0, tiled=True)
+        got = row_stats(piece, head_t, wanted[:, lo:hi].reshape(-1))
+        parts.append(got.reshape(4, n_voc, hi - lo))
+    stats = jnp.concatenate(parts, axis=2).reshape(4, group_rows)
     every = lax.all_gather(stats, "voc", axis=0)
     top = jnp.max(every[:, 0], axis=0)
     factor = jnp.exp(every[:, 0] - top[None, :])
@@ -148,8 +151,7 @@
     device = lax.axis_index(("tok", "voc"))
     positions = device * out_rows + jnp.arange(out_rows, dtype=jnp.int32)
     rows = slot_rows(positions, lengths, perm)
-    picked_out = jnp.take(both, rows, axis=1)
-    return (picked_out[0], picked_out[1])
+    return (both[0][rows], both[1][rows])
 
 
 def solution(mesh):

time: 229 us -> 204 us (0.89)
  blocking collectives: 55.5 us -> 22.2 us
  waiting for transfers between devices: 48.5 us -> 36.1 us
  Pallas kernels: 98.1 us -> 106 us
  local copies, waits for them, and re-layouts: 4.46 us -> 11.1 us
  other arithmetic: 7.98 us -> 13.4 us
    all_gather x1, blocking collectives: 41.3 us -> 8.04 us  [on_device(): both = lax.all_gather(own, 'tok', axis=1, tiled=True)]
    all_gather x2 -> x3, waiting for transfers between devices: 47.8 us -> 36.1 us  [on_device(): piece = lax.all_gather(normed, 'voc', axis=0, tiled=True)]
    pallas_call x2 -> x3, Pallas kernels: 98.1 us -> 106 us  [row_stats(): pl.pallas_call(lambda *refs: stats_kernel(ncols, *refs), grid=(rows // tm...]
    unnamed x4 -> x10, local copies, waits for them, and re-layouts: 0.01 us -> 5.38 us
    convert_element_type x1 -> x3, other arithmetic: 2.57 us -> 5.7 us  [norm(): (values * scale * gain.astype(jnp.float32)[None, :]).astype(jnp.bfloat16)]
  transfers between devices with their start and end apart: 2 -> 3, of which waited for: 1 -> 2; matrix products, arithmetic and copies ran while one was open for 1% -> 5% of each run, Pallas kernels for 21% -> 32%
where the time goes in v9:
time: 204 us; the launch traced here: 203 us
  Pallas kernels  106 us (52%)
  waiting for transfers between devices  36.1 us (18%)
  blocking collectives  22.2 us (11%)
  between operations  14 us (7%)
  other arithmetic  13.4 us (7%)
  local copies, waits for them, and re-layouts  11.1 us (5%)
    pallas_call x3, Pallas kernels, row_stats(): pl.pallas_call(lambda *refs: stats_kernel(ncols, *refs), grid=(rows // tm...  106 us
    all_gather x3, waiting for transfers between devices, on_device(): piece = lax.all_gather(normed, 'voc', axis=0, tiled=True)  36.1 us
    all_gather x1, blocking collectives, on_device(): every = lax.all_gather(stats, 'voc', axis=0)  14.2 us
    all_gather x1, blocking collectives, on_device(): both = lax.all_gather(own, 'tok', axis=1, tiled=True)  8.04 us
    convert_element_type x3, other arithmetic, norm(): (values * scale * gain.astype(jnp.float32)[None, :]).astype(jnp.bfloat16)  5.7 us
    unnamed x10, local copies, waits for them, and re-layouts  5.38 us
  transfers between devices with their start and end apart: 3, of which 2 were waited for; matrix products, arithmetic and copies ran while one was open for 5% of the time, Pallas kernels for 32%

profile of v9, /device:TPU:0, one launch (start us, length us, event | category | flops | bytes accessed | tf_op | source)
XLA Modules:
  0.0 202.6 jit_solution(12192616753559357714)
XLA Ops:
  7.2 1.1 fusion.6
  8.3 0.7 convert_element_type.27
  9.0 1.8 fusion.8
  10.9 1.2 fusion
  12.1 1.9 fusion.2
  14.1 1.2 fusion.3
  15.3 2.0 fusion.5
  17.3 0.2 reduce-window.9
  17.5 0.7 dynamic-slice_subtract_fusion
  18.2 0.1 reshape.224
  18.4 0.1 reshape.225
  18.4 0.1 reshape.226
  18.5 0.1 convert_reduce_fusion
  18.6 0.1 select_reduce_fusion.1
  18.8 24.1 %all-gather.4.cloned.1.call-done.refs_0_ = bf16[512,2048]{1,0:T(8,128)(2,1)} async-done(((bf16[64,2048]{1,0:T(8,128)(2,1)}), bf16[512,2048]{1,0:T(8,128)(2,1)}) %all-gather.4.cloned.1.call-update) | async-done | bytes 2097168 | tf_op jit(solution)/shard_map/all_gather | solution.py:137
  42.9 0.1 broadcast_in_dim.30.refs_2_
  43.0 1.6 copy-done.2
  44.6 24.7 %shard_map.77 = (f32[512,1]{1,0:T(8,128)S(1)}, f32[512,1]{1,0:T(8,128)S(1)}, f32[512,1]{1,0:T(8,128)S(1)}, f32[512,1]{1,0:T(8,128)S(1)}) custom-call(bf16[512,2048]{1,0:T(8,128)(2,1)S(1)} %copy-done.2, bf16[6288,2048]{1,0:T(8,128)(2,1)} %bitcast.38, s32[512,128]{1,0:T(8,128)S(1)} %broadcast_in_dim.30.refs_2_), custom_call_target="tpu_custom_call" | custom-call | flops 13186891776 | bytes 27852800 | tf_op jit(solution)/shard_map/pallas_call | solution.py:91
  69.3 0.1 reduce.2
  69.5 0.1 stack.38
  69.5 0.1 reduce.3
  69.7 0.1 stack.39
  69.8 0.1 reduce.4
  69.9 0.1 stack.40
  70.0 0.1 reduce.5
  70.2 0.1 stack.41
  70.2 12.0 %all-gather.6.cloned.1.call-done.refs_0_ = bf16[768,2048]{1,0:T(8,128)(2,1)} async-done(((bf16[96,2048]{1,0:T(8,128)(2,1)}), bf16[768,2048]{1,0:T(8,128)(2,1)}) %all-gather.6.cloned.1.call-update) | async-done | bytes 3145744 | tf_op jit(solution)/shard_map/all_gather | solution.py:137
  82.2 0.2 broadcast_in_dim.36.refs_2_
  82.4 1.9 copy-done.1
  84.2 40.6 %shard_map.78 = (f32[768,1]{1,0:T(8,128)S(1)}, f32[768,1]{1,0:T(8,128)S(1)}, f32[768,1]{1,0:T(8,128)S(1)}, f32[768,1]{1,0:T(8,128)S(1)}) custom-call(bf16[768,2048]{1,0:T(8,128)(2,1)S(1)} %copy-done.1, bf16[6288,2048]{1,0:T(8,128)(2,1)} %bitcast.39, s32[768,128]{1,0:T(8,128)S(1)} %broadcast_in_dim.36.refs_2_), custom_call_target="tpu_custom_call" | custom-call | flops 19780337664 | bytes 54657024 | tf_op jit(solution)/shard_map/pallas_call | solution.py:91
  124.9 0.2 reduce.6
  125.1 0.2 reduce.7
  125.4 0.2 reduce.8
  125.6 0.2 reduce.9
  125.9 0.2 broadcast_in_dim.37.refs_2_
  126.1 1.9 copy-done
  127.9 40.2 %shard_map.79 = (f32[768,1]{1,0:T(8,128)S(1)}, f32[768,1]{1,0:T(8,128)S(1)}, f32[768,1]{1,0:T(8,128)S(1)}, f32[768,1]{1,0:T(8,128)S(1)}) custom-call(bf16[768,2048]{1,0:T(8,128)(2,1)S(1)} %copy-done, bf16[6288,2048]{1,0:T(8,128)(2,1)} %bitcast.40, s32[768,128]{1,0:T(8,128)S(1)} %broadcast_in_dim.37.refs_2_), custom_call_target="tpu_custom_call" | custom-call | flops 19780337664 | bytes 54657024 | tf_op jit(solution)/shard_map/pallas_call | solution.py:91
  168.2 0.2 reduce.10
  168.4 0.2 reduce.11
  168.7 0.2 reduce.12
  168.9 0.2 reduce.13
  169.2 0.1 maximum_maximum_fusion
  169.3 14.2 %all_gather.18 = f32[8,4,2048]{2,1,0:T(4,128)S(1)} all-gather(f32[1,4,2048]{2,1,0:T(4,128)S(1)} %all_gather_reshape.3), channel_id=1, replica_groups=mesh['tok'=4,'voc'=8] {'voc'}, dimensions={0}, use_global_device_ids=true | all-gather | bytes 294912 | tf_op jit(solution)/shard_map/all_gather | solution.py:141
  183.5 0.2 fusion.15
  183.7 0.1 fusion.10
  183.9 8.0 %all_gather.19 = f32[2,8192]{1,0:T(2,128)S(1)} all-gather(f32[2,2048]{1,0:T(2,128)S(1)} %pad_maximum_fusion), channel_id=1, replica_groups=mesh['tok'=4,'voc'=8] {'tok'}, dimensions={1}, use_global_device_ids=true | all-gather | bytes 81920 | tf_op jit(solution)/shard_map/all_gather | solution.py:149
  192.0 2.0 gather_fusion.1
  194.0 2.0 gather_fusion
  (41 shorter events, 1.0 us)
Async XLA Ops:
  7.2 10.2 %copy-start.4 = (s32[8]{0:T(128)S(1)}, s32[8]{0:T(128)}, u32[]{:S(2)}) copy-start(s32[8]{0:T(128)} %param.10) | copy-start | bytes 100
  7.2 11.5 %copy-start.3 = (s32[8]{0:T(128)S(1)}, s32[8]{0:T(128)}, u32[]{:S(2)}) copy-start(s32[8]{0:T(128)} %param.11) | copy-start | bytes 100
  7.2 35.7 %all-gather.4.cloned.1.call-start = ((), (), s32[]{:S(2)}) async-start(), calls=%async_computation | async-start | bytes 2359296 | tf_op jit(solution)/shard_map/all_gather | solution.py:137
  10.9 71.3 %all-gather.6.cloned.1.call-start = ((), (), s32[]{:S(2)}) async-start(), calls=%async_computation.1 | async-start | bytes 3538944 | tf_op jit(solution)/shard_map/all_gather | solution.py:137
  14.1 111.8 %all-gather.8.cloned.1.call-start = ((), (), s32[]{:S(2)}) async-start(), calls=%async_computation.2 | async-start | bytes 3538944 | tf_op jit(solution)/shard_map/all_gather | solution.py:137
  43.0 1.6 copy-start.2
  82.3 1.9 copy-start.1
  126.0 1.9 copy-start
Sparse Core Ops, SparseCore 0:
  11.0 31.8 all-gather.3
  44.5 37.5 all-gather.5
  83.8 37.4 all-gather.7

commit v10 on v5

--- a/solution.py
+++ b/solution.py
@@ -146,7 +146,10 @@
     device = lax.axis_index(("tok", "voc"))
     positions = device * out_rows + jnp.arange(out_rows, dtype=jnp.int32)
     rows = slot_rows(positions, lengths, perm)
-    return (both[0][rows], both[1][rows])
+    hit = rows[:, None] == jnp.arange(both.shape[1], dtype=jnp.int32)[None, :]
+    lp = jnp.sum(jnp.where(hit, both[0][None, :], 0.0), axis=1)
+    ent = jnp.sum(jnp.where(hit, both[1][None, :], 0.0), axis=1)
+    return (lp, ent)
 
 
 def solution(mesh):

time: 196 us -> 194 us (0.990)
  local copies, waits for them, and re-layouts: 5.73 us -> 1.68 us
  other arithmetic: 6.87 us -> 9.14 us
    gather x2 -> x0, local copies, waits for them, and re-layouts: 4.05 us -> none  [on_device(): return (both[0][rows], both[1][rows])]
    reduce_sum x0 -> x1, other arithmetic: none -> 2.29 us  [on_device(): ent = jnp.sum(jnp.where(hit, both[1][None, :], 0.0), axis=1)]
where the time goes in v10:
time: 194 us
  Pallas kernels  98.1 us (51%)
  waiting for transfers between devices  48.6 us (25%)
  blocking collectives  22.3 us (11%)
  between operations  14.2 us (7%)
  other arithmetic  9.14 us (5%)
    pallas_call x2, Pallas kernels, row_stats(): pl.pallas_call(lambda *refs: stats_kernel(ncols, *refs), grid=(rows // tm...  98.1 us
    all_gather x2, waiting for transfers between devices, on_device(): lax.all_gather(normed[j * step:(j + 1) * step], 'voc', axis=0, tiled=True)  47.9 us
    all_gather x1, blocking collectives, on_device(): every = lax.all_gather(stats, 'voc', axis=0)  14.2 us
    all_gather x1, blocking collectives, on_device(): both = lax.all_gather(own, 'tok', axis=1, tiled=True)  8.12 us
  transfers between devices with their start and end apart: 2, of which 1 were waited for; matrix products, arithmetic and copies ran while one was open for 1% of the time, Pallas kernels for 25%

profile of v10, /device:TPU:0, one launch (start us, length us, event | category | flops | bytes accessed | tf_op | source)
XLA Modules:
  0.0 194.1 jit_solution(2074842710912326812)
XLA Ops:
  7.2 0.0 copy-start.1
  7.2 0.0 copy-start
  7.2 0.0 all-gather.3.cloned.1.call-start
  7.2 0.7 convert_element_type.14
  7.9 1.5 fusion
  9.4 1.5 fusion.2
  11.0 1.2 fusion.9
  12.2 0.0 all-gather.3.cloned.1.call-update
  12.2 0.0 all-gather.5.cloned.1.call-start
  12.2 0.7 all-gather.5.cloned.1.call-update
  12.9 0.0 copy-done.1
  13.0 0.2 reduce-window.9
  13.1 0.7 dynamic-slice_subtract_fusion
  13.8 0.1 convert_reduce_fusion
  13.9 0.0 copy-done
  14.0 0.1 select_reduce_fusion.3
  14.1 47.8 %all-gather.3.cloned.1.call-done.refs_0_ = bf16[1024,2048]{1,0:T(8,128)(2,1)} async-done(((bf16[128,2048]{1,0:T(8,128)(2,1)}), bf16[1024,2048]{1,0:T(8,128)(2,1)}) %all-gather.3.cloned.1.call-update) | async-done | bytes 4194320 | tf_op jit(solution)/shard_map/all_gather | solution.py:133
  61.9 0.2 broadcast_in_dim.74.refs_2_
  62.1 49.1 %shard_map.77 = (f32[1024,1]{1,0:T(8,128)S(1)}, f32[1024,1]{1,0:T(8,128)S(1)}, f32[1024,1]{1,0:T(8,128)S(1)}, f32[1024,1]{1,0:T(8,128)S(1)}) custom-call(bf16[1024,2048]{1,0:T(8,128)(2,1)} %all-gather.3.cloned.1.call-done.refs_0_, bf16[6288,2048]{1,0:T(8,128)(2,1)} %bitcast.54, s32[1024,128]{1,0:T(8,128)S(1)} %broadcast_in_dim.74.refs_2_), custom_call_target="tpu_custom_call" | custom-call | flops 26373783552 | bytes 55705600 | tf_op jit(solution)/shard_map/pallas_call | solution.py:92
  111.3 0.2 reduce.2
  111.5 0.2 reduce.3
  111.7 0.2 reduce.4
  111.9 0.2 reduce.5
  112.1 0.0 all-gather.5.cloned.1.call-done.refs_0_
  112.1 0.2 broadcast_in_dim.75.refs_2_
  112.3 49.0 %shard_map.78 = (f32[1024,1]{1,0:T(8,128)S(1)}, f32[1024,1]{1,0:T(8,128)S(1)}, f32[1024,1]{1,0:T(8,128)S(1)}, f32[1024,1]{1,0:T(8,128)S(1)}) custom-call(bf16[1024,2048]{1,0:T(8,128)(2,1)} %all-gather.5.cloned.1.call-done.refs_0_, bf16[6288,2048]{1,0:T(8,128)(2,1)} %bitcast.55, s32[1024,128]{1,0:T(8,128)S(1)} %broadcast_in_dim.75.refs_2_), custom_call_target="tpu_custom_call" | custom-call | flops 26373783552 | bytes 55705600 | tf_op jit(solution)/shard_map/pallas_call | solution.py:92
  161.3 0.2 reduce.6
  161.5 0.2 reduce.7
  161.7 0.2 reduce.8
  161.9 0.2 reduce.9
  162.2 14.2 %all_gather.14 = f32[8,4,2048]{2,1,0:T(4,128)S(1)} all-gather(f32[1,4,2048]{2,1,0:T(4,128)S(1)} %all_gather_reshape.3), channel_id=1, replica_groups=mesh['tok'=4,'voc'=8] {'voc'}, dimensions={0}, use_global_device_ids=true | all-gather | bytes 294912 | tf_op jit(solution)/shard_map/all_gather | solution.py:136
  176.4 0.2 fusion.10
  176.7 0.1 fusion.4
  176.8 8.1 %all_gather.15 = f32[2,8192]{1,0:T(2,128)S(1)} all-gather(f32[2,2048]{1,0:T(2,128)S(1)} %pad_maximum_fusion), channel_id=1, replica_groups=mesh['tok'=4,'voc'=8] {'tok'}, dimensions={1}, use_global_device_ids=true | all-gather | bytes 81920 | tf_op jit(solution)/shard_map/all_gather | solution.py:144
  184.9 0.1 fusion.11
  185.0 2.3 %select_reduce_fusion = (f32[160]{0:T(256)}, f32[160]{0:T(256)}) fusion(f32[8192]{0:T(1024)S(1)} %bitcast.40, s32[160]{0:T(256)S(1)} %add_subtract_fusion, f32[8192]{0:T(1024)S(1)} %bitcast.39), kind=kLoop, calls=%fused_computation | loop fusion | flops 6553280 | bytes 67456 | tf_op jit(solution)/shard_map/reduce_sum | solution.py:151
  (13 shorter events, 0.1 us)
Async XLA Ops:
  7.2 5.8 %copy-start.1 = (s32[8]{0:T(128)S(1)}, s32[8]{0:T(128)}, u32[]{:S(2)}) copy-start(s32[8]{0:T(128)} %param.10) | copy-start | bytes 100
  7.2 6.8 %copy-start = (s32[8]{0:T(128)S(1)}, s32[8]{0:T(128)}, u32[]{:S(2)}) copy-start(s32[8]{0:T(128)} %param.11) | copy-start | bytes 100
  7.2 54.7 %all-gather.3.cloned.1.call-start = ((), (), s32[]{:S(2)}) async-start(), calls=%async_computation | async-start | bytes 4718592 | tf_op jit(solution)/shard_map/all_gather | solution.py:133
  12.2 99.9 %all-gather.5.cloned.1.call-start = ((), (), s32[]{:S(2)}) async-start(), calls=%async_computation.1 | async-start | bytes 4718592 | tf_op jit(solution)/shard_map/all_gather | solution.py:133
Sparse Core Ops, SparseCore 0:
  12.3 49.5 all-gather.2
  63.5 45.6 all-gather.4

commit v11 on v10

--- a/solution.py
+++ b/solution.py
@@ -83,7 +83,7 @@
 def row_stats(piece, weights_t, wanted):
     rows, depth = piece.shape
     ncols = weights_t.shape[0]
-    tm = min(512, rows)
+    tm = min(1024, rows)
     tn = TILE_N
     lane = 128
     steps = pl.cdiv(ncols, tn)

time: 194 us -> 189 us (0.974)
  Pallas kernels: 98.1 us -> 91.8 us
    pallas_call x2, Pallas kernels: 98.1 us -> 91.8 us  [row_stats(): pl.pallas_call(lambda *refs: stats_kernel(ncols, *refs), grid=(rows // tm...]
  transfers between devices with their start and end apart: 2 -> 2, of which waited for: 1 -> 2; matrix products, arithmetic and copies ran while one was open for 1% -> 1% of each run, Pallas kernels for 25% -> 24%
where the time goes in v11:
time: 189 us; the launch traced here: 188 us
  Pallas kernels  91.8 us (49%)
  waiting for transfers between devices  48.9 us (26%)
  blocking collectives  22.4 us (12%)
  between operations  14.2 us (8%)
  other arithmetic  9.14 us (5%)
    pallas_call x2, Pallas kernels, row_stats(): pl.pallas_call(lambda *refs: stats_kernel(ncols, *refs), grid=(rows // tm...  91.8 us
    all_gather x2, waiting for transfers between devices, on_device(): lax.all_gather(normed[j * step:(j + 1) * step], 'voc', axis=0, tiled=True)  48.2 us
    all_gather x1, blocking collectives, on_device(): every = lax.all_gather(stats, 'voc', axis=0)  14.2 us
    all_gather x1, blocking collectives, on_device(): both = lax.all_gather(own, 'tok', axis=1, tiled=True)  8.19 us
  transfers between devices with their start and end apart: 2, of which 2 were waited for; matrix products, arithmetic and copies ran while one was open for 1% of the time, Pallas kernels for 24%

profile of v11, /device:TPU:0, one launch (start us, length us, event | category | flops | bytes accessed | tf_op | source)
XLA Modules:
  0.0 188.2 jit_solution(6621947725503087019)
XLA Ops:
  7.2 0.0 copy-start.1
  7.2 0.0 copy-start
  7.2 0.0 all-gather.3.cloned.1.call-start
  7.2 0.7 convert_element_type.14
  7.9 1.5 fusion
  9.4 1.5 fusion.2
  11.0 1.2 fusion.9
  12.2 0.0 all-gather.3.cloned.1.call-update
  12.2 0.0 all-gather.5.cloned.1.call-start
  12.2 0.7 all-gather.5.cloned.1.call-update
  12.9 0.0 copy-done.1
  13.0 0.2 reduce-window.9
  13.1 0.7 dynamic-slice_subtract_fusion
  13.8 0.1 convert_reduce_fusion
  13.9 0.0 copy-done
  14.0 0.1 select_reduce_fusion.3
  14.1 47.8 %all-gather.3.cloned.1.call-done.refs_0_ = bf16[1024,2048]{1,0:T(8,128)(2,1)} async-done(((bf16[128,2048]{1,0:T(8,128)(2,1)}), bf16[1024,2048]{1,0:T(8,128)(2,1)}) %all-gather.3.cloned.1.call-update) | async-done | bytes 4194320 | tf_op jit(solution)/shard_map/all_gather | solution.py:133
  61.9 0.2 broadcast_in_dim.74.refs_2_
  62.1 45.9 %shard_map.77 = (f32[1024,1]{1,0:T(8,128)S(1)}, f32[1024,1]{1,0:T(8,128)S(1)}, f32[1024,1]{1,0:T(8,128)S(1)}, f32[1024,1]{1,0:T(8,128)S(1)}) custom-call(bf16[1024,2048]{1,0:T(8,128)(2,1)} %all-gather.3.cloned.1.call-done.refs_0_, bf16[6288,2048]{1,0:T(8,128)(2,1)} %bitcast.54, s32[1024,128]{1,0:T(8,128)S(1)} %broadcast_in_dim.74.refs_2_), custom_call_target="tpu_custom_call" | custom-call | flops 26373783552 | bytes 29949952 | tf_op jit(solution)/shard_map/pallas_call | solution.py:92
  108.0 0.2 reduce.2
  108.2 0.2 reduce.3
  108.5 0.2 reduce.4
  108.7 0.2 reduce.5
  108.9 0.4 all-gather.5.cloned.1.call-done.refs_0_
  109.2 0.2 broadcast_in_dim.75.refs_2_
  109.4 45.9 %shard_map.78 = (f32[1024,1]{1,0:T(8,128)S(1)}, f32[1024,1]{1,0:T(8,128)S(1)}, f32[1024,1]{1,0:T(8,128)S(1)}, f32[1024,1]{1,0:T(8,128)S(1)}) custom-call(bf16[1024,2048]{1,0:T(8,128)(2,1)} %all-gather.5.cloned.1.call-done.refs_0_, bf16[6288,2048]{1,0:T(8,128)(2,1)} %bitcast.55, s32[1024,128]{1,0:T(8,128)S(1)} %broadcast_in_dim.75.refs_2_), custom_call_target="tpu_custom_call" | custom-call | flops 26373783552 | bytes 29949952 | tf_op jit(solution)/shard_map/pallas_call | solution.py:92
  155.3 0.2 reduce.6
  155.5 0.2 reduce.7
  155.8 0.2 reduce.8
  156.0 0.2 reduce.9
  156.3 14.2 %all_gather.14 = f32[8,4,2048]{2,1,0:T(4,128)S(1)} all-gather(f32[1,4,2048]{2,1,0:T(4,128)S(1)} %all_gather_reshape.3), channel_id=1, replica_groups=mesh['tok'=4,'voc'=8] {'voc'}, dimensions={0}, use_global_device_ids=true | all-gather | bytes 294912 | tf_op jit(solution)/shard_map/all_gather | solution.py:136
  170.5 0.2 fusion.10
  170.7 0.1 fusion.4
  170.9 8.2 %all_gather.15 = f32[2,8192]{1,0:T(2,128)S(1)} all-gather(f32[2,2048]{1,0:T(2,128)S(1)} %pad_maximum_fusion), channel_id=1, replica_groups=mesh['tok'=4,'voc'=8] {'tok'}, dimensions={1}, use_global_device_ids=true | all-gather | bytes 81920 | tf_op jit(solution)/shard_map/all_gather | solution.py:144
  179.0 0.1 fusion.11
  179.1 2.3 %select_reduce_fusion = (f32[160]{0:T(256)}, f32[160]{0:T(256)}) fusion(f32[8192]{0:T(1024)S(1)} %bitcast.40, s32[160]{0:T(256)S(1)} %add_subtract_fusion, f32[8192]{0:T(1024)S(1)} %bitcast.39), kind=kLoop, calls=%fused_computation | loop fusion | flops 6553280 | bytes 67456 | tf_op jit(solution)/shard_map/reduce_sum | solution.py:151
  (13 shorter events, 0.1 us)
Async XLA Ops:
  7.2 5.8 %copy-start.1 = (s32[8]{0:T(128)S(1)}, s32[8]{0:T(128)}, u32[]{:S(2)}) copy-start(s32[8]{0:T(128)} %param.10) | copy-start | bytes 100
  7.2 6.8 %copy-start = (s32[8]{0:T(128)S(1)}, s32[8]{0:T(128)}, u32[]{:S(2)}) copy-start(s32[8]{0:T(128)} %param.11) | copy-start | bytes 100
  7.2 54.7 %all-gather.3.cloned.1.call-start = ((), (), s32[]{:S(2)}) async-start(), calls=%async_computation | async-start | bytes 4718592 | tf_op jit(solution)/shard_map/all_gather | solution.py:133
  12.2 97.1 %all-gather.5.cloned.1.call-start = ((), (), s32[]{:S(2)}) async-start(), calls=%async_computation.1 | async-start | bytes 4718592 | tf_op jit(solution)/shard_map/all_gather | solution.py:133
Sparse Core Ops, SparseCore 0:
  12.3 49.5 all-gather.2
  63.5 45.6 all-gather.4

commit v12 on v11

--- a/solution.py
+++ b/solution.py
@@ -7,7 +7,7 @@
 
 MAXLEN = 1024
 CHUNKS = 2
-TILE_N = 512
+TILE_N = 768
 NEG = -1e30
 
 

time: 189 us -> 190 us (level)
  transfers between devices with their start and end apart: 2 -> 2, of which waited for: 2 -> 1; matrix products, arithmetic and copies ran while one was open for 1% -> 1% of each run, Pallas kernels for 24% -> 25%
where the time goes in v12:
time: 190 us; the launch traced here: 189 us
  Pallas kernels  93.4 us (49%)
  waiting for transfers between devices  48.6 us (26%)
  blocking collectives  22.4 us (12%)
  between operations  14.2 us (7%)
  other arithmetic  9.14 us (5%)
    pallas_call x2, Pallas kernels, row_stats(): pl.pallas_call(lambda *refs: stats_kernel(ncols, *refs), grid=(rows // tm...  93.4 us
    all_gather x2, waiting for transfers between devices, on_device(): lax.all_gather(normed[j * step:(j + 1) * step], 'voc', axis=0, tiled=True)  47.9 us
    all_gather x1, blocking collectives, on_device(): every = lax.all_gather(stats, 'voc', axis=0)  14.2 us
    all_gather x1, blocking collectives, on_device(): both = lax.all_gather(own, 'tok', axis=1, tiled=True)  8.19 us
  transfers between devices with their start and end apart: 2, of which 1 were waited for; matrix products, arithmetic and copies ran while one was open for 1% of the time, Pallas kernels for 25%

profile of v12, /device:TPU:0, one launch (start us, length us, event | category | flops | bytes accessed | tf_op | source)
XLA Modules:
  0.0 189.5 jit_solution(7067883865575382662)
XLA Ops:
  7.2 0.0 copy-start.1
  7.2 0.0 copy-start
  7.2 0.0 all-gather.3.cloned.1.call-start
  7.2 0.7 convert_element_type.14
  7.9 1.5 fusion
  9.4 1.5 fusion.2
  11.0 1.2 fusion.9
  12.2 0.0 all-gather.3.cloned.1.call-update
  12.2 0.0 all-gather.5.cloned.1.call-start
  12.2 0.7 all-gather.5.cloned.1.call-update
  12.9 0.0 copy-done.1
  13.0 0.2 reduce-window.9
  13.1 0.7 dynamic-slice_subtract_fusion
  13.8 0.1 convert_reduce_fusion
  13.9 0.0 copy-done
  14.0 0.1 select_reduce_fusion.3
  14.1 47.8 %all-gather.3.cloned.1.call-done.refs_0_ = bf16[1024,2048]{1,0:T(8,128)(2,1)} async-done(((bf16[128,2048]{1,0:T(8,128)(2,1)}), bf16[1024,2048]{1,0:T(8,128)(2,1)}) %all-gather.3.cloned.1.call-update) | async-done | bytes 4194320 | tf_op jit(solution)/shard_map/all_gather | solution.py:133
  61.9 0.2 broadcast_in_dim.74.refs_2_
  62.1 46.6 %shard_map.77 = (f32[1024,1]{1,0:T(8,128)S(1)}, f32[1024,1]{1,0:T(8,128)S(1)}, f32[1024,1]{1,0:T(8,128)S(1)}, f32[1024,1]{1,0:T(8,128)S(1)}) custom-call(bf16[1024,2048]{1,0:T(8,128)(2,1)} %all-gather.3.cloned.1.call-done.refs_0_, bf16[6288,2048]{1,0:T(8,128)(2,1)} %bitcast.54, s32[1024,128]{1,0:T(8,128)S(1)} %broadcast_in_dim.74.refs_2_), custom_call_target="tpu_custom_call" | custom-call | flops 26373783552 | bytes 29949952 | tf_op jit(solution)/shard_map/pallas_call | solution.py:92
  108.7 0.2 reduce.2
  109.0 0.2 reduce.3
  109.2 0.2 reduce.4
  109.4 0.2 reduce.5
  109.6 0.0 all-gather.5.cloned.1.call-done.refs_0_
  109.6 0.2 broadcast_in_dim.75.refs_2_
  109.8 46.8 %shard_map.78 = (f32[1024,1]{1,0:T(8,128)S(1)}, f32[1024,1]{1,0:T(8,128)S(1)}, f32[1024,1]{1,0:T(8,128)S(1)}, f32[1024,1]{1,0:T(8,128)S(1)}) custom-call(bf16[1024,2048]{1,0:T(8,128)(2,1)} %all-gather.5.cloned.1.call-done.refs_0_, bf16[6288,2048]{1,0:T(8,128)(2,1)} %bitcast.55, s32[1024,128]{1,0:T(8,128)S(1)} %broadcast_in_dim.75.refs_2_), custom_call_target="tpu_custom_call" | custom-call | flops 26373783552 | bytes 29949952 | tf_op jit(solution)/shard_map/pallas_call | solution.py:92
  156.6 0.2 reduce.6
  156.8 0.2 reduce.7
  157.0 0.2 reduce.8
  157.2 0.2 reduce.9
  157.5 14.2 %all_gather.14 = f32[8,4,2048]{2,1,0:T(4,128)S(1)} all-gather(f32[1,4,2048]{2,1,0:T(4,128)S(1)} %all_gather_reshape.3), channel_id=1, replica_groups=mesh['tok'=4,'voc'=8] {'voc'}, dimensions={0}, use_global_device_ids=true | all-gather | bytes 294912 | tf_op jit(solution)/shard_map/all_gather | solution.py:136
  171.7 0.2 fusion.10
  172.0 0.1 fusion.4
  172.1 8.2 %all_gather.15 = f32[2,8192]{1,0:T(2,128)S(1)} all-gather(f32[2,2048]{1,0:T(2,128)S(1)} %pad_maximum_fusion), channel_id=1, replica_groups=mesh['tok'=4,'voc'=8] {'tok'}, dimensions={1}, use_global_device_ids=true | all-gather | bytes 81920 | tf_op jit(solution)/shard_map/all_gather | solution.py:144
  180.3 0.1 fusion.11
  180.4 2.3 %select_reduce_fusion = (f32[160]{0:T(256)}, f32[160]{0:T(256)}) fusion(f32[8192]{0:T(1024)S(1)} %bitcast.40, s32[160]{0:T(256)S(1)} %add_subtract_fusion, f32[8192]{0:T(1024)S(1)} %bitcast.39), kind=kLoop, calls=%fused_computation | loop fusion | flops 6553280 | bytes 67456 | tf_op jit(solution)/shard_map/reduce_sum | solution.py:151
  (13 shorter events, 0.1 us)
Async XLA Ops:
  7.2 5.8 %copy-start.1 = (s32[8]{0:T(128)S(1)}, s32[8]{0:T(128)}, u32[]{:S(2)}) copy-start(s32[8]{0:T(128)} %param.10) | copy-start | bytes 100
  7.2 6.8 %copy-start = (s32[8]{0:T(128)S(1)}, s32[8]{0:T(128)}, u32[]{:S(2)}) copy-start(s32[8]{0:T(128)} %param.11) | copy-start | bytes 100
  7.2 54.7 %all-gather.3.cloned.1.call-start = ((), (), s32[]{:S(2)}) async-start(), calls=%async_computation | async-start | bytes 4718592 | tf_op jit(solution)/shard_map/all_gather | solution.py:133
  12.2 97.4 %all-gather.5.cloned.1.call-start = ((), (), s32[]{:S(2)}) async-start(), calls=%async_computation.1 | async-start | bytes 4718592 | tf_op jit(solution)/shard_map/all_gather | solution.py:133
Sparse Core Ops, SparseCore 0:
  12.3 49.5 all-gather.2
  63.5 45.6 all-gather.4
